TPU v7x, 256 devices: a whole 4x4x8 slice. The times are simulated.
256 devices in a mesh: req: 8 (over z), seq: 32 (over y, x, core).
Axes of the slice: x: 4, y: 4, z: 8, core: 2. Of those that a mesh axis runs over, the one named last changes fastest.
Arguments:
- hidden_in: bfloat16 [16, 1024, 2048], P('req', 'seq'), may hold values from -6 to 6
- norm_gain: float32 [2048], replicated, may hold values from 0.1 to 1.9
- w_query: bfloat16 [2048, 1024], P(('req', 'seq')), may hold values from -0.125 to 0.125
- w_key: bfloat16 [2048, 512], P(('req', 'seq')), may hold values from -0.3125 to 0.3125
- w_value: bfloat16 [2048, 512], P(('req', 'seq')), may hold values from -0.125 to 0.125
- cache_keys: bfloat16 [16, 8192, 512], P('req', 'seq'), may hold values from -525 to 525
- cache_values: bfloat16 [16, 8192, 512], P('req', 'seq'), may hold values from -6 to 6
- cache_lengths: int32 [16], P('req'), may hold values from 1 to 8192, as said below
Outputs:
- attended: bfloat16 [16, 1024, 1024], P('req', 'seq')
- new_keys: bfloat16 [16, 1024, 512], P('req', 'seq')
- new_values: bfloat16 [16, 1024, 512], P('req', 'seq')
Inputs may be any that keep to these rules, and one draw needn't show every extreme that they name: `cache_lengths`: some request's cache holds exactly 8192 positions.
All inputs are finite; a program needn't handle non-finite values.
Results may differ from a plain program's by a relative error of at most 0.034.
Values may be sent and summed in bfloat16 or wider, within the bound.
No kernel may reach another device: no remote copies, remote signals or barrier semaphores. Data moves between devices by JAX's collectives and lax.ppermute only.
A program may use at most 128 MiB of HBM per device.

v0:
```python
import jax
import jax.numpy as jnp
from jax import lax
from jax.sharding import PartitionSpec as P

HEADS = 4
KV_HEADS = 2
HEAD = 256


EPSILON = 1e-06
THETA = 1000042.0
MASKED = -1e30


def tables(positions, head_size):
    half_size = head_size // 2
    frequency = THETA ** (-(jnp.arange(half_size, dtype=jnp.float32) * 2.0 / head_size))
    angles = positions.astype(jnp.float32)[..., None] * frequency
    return (jnp.cos(angles)[..., None, :], jnp.sin(angles)[..., None, :])


def rotate(values, cosine, sine_part):
    half_size = values.shape[-1] // 2
    first_half = values[..., :half_size]
    second_half = values[..., half_size:]
    return jnp.concatenate(
        [
            first_half * cosine - second_half * sine_part,
            second_half * cosine + first_half * sine_part,
        ],
        axis=-1,
    )


def attend(query_rows, key_rows, value_rows, live):
    span_len = query_rows.shape[0]
    group_size = HEADS // KV_HEADS
    query_view = query_rows.reshape(span_len, KV_HEADS, group_size, HEAD)
    key_view = key_rows.reshape(key_rows.shape[0], KV_HEADS, HEAD)
    value_view = value_rows.reshape(value_rows.shape[0], KV_HEADS, HEAD)
    scores = jnp.einsum(
        "cgeh,kgh->cgek", query_view, key_view, preferred_element_type=jnp.float32
    ) * HEAD ** (-0.5)
    mask_view = live[:, None, None, :]
    scores = jnp.where(mask_view, scores, MASKED)
    block_max = jnp.max(scores, axis=-1)
    weights = jnp.where(mask_view, jnp.exp(scores - block_max[..., None]), 0.0)
    block_sum = jnp.sum(weights, axis=-1)
    block_out = jnp.einsum(
        "cgek,kgh->cgeh",
        weights.astype(jnp.bfloat16),
        value_view,
        preferred_element_type=jnp.float32,
    )
    return (
        block_max.reshape(span_len, HEADS),
        block_sum.reshape(span_len, HEADS),
        block_out.reshape(span_len, HEADS * HEAD).astype(jnp.bfloat16),
    )


def attend_rows(query_rows, key_rows, value_rows, live):
    total_rows = query_rows.shape[0]
    row_block = min(512, total_rows)
    pieces = []
    for begin in range(0, total_rows, row_block):
        pieces.append(
            attend(
                query_rows[begin : begin + row_block],
                key_rows,
                value_rows,
                live[begin : begin + row_block],
            )
        )
    return tuple((jnp.concatenate([piece[slot] for piece in pieces], axis=0) for slot in range(3)))


def body(hidden_in, norm_gain, w_query, w_key, w_value, cache_keys, cache_values, cache_lengths):
    seq_count = lax.axis_size("seq")
    seq_seat = lax.axis_index("seq")
    req_local, slice_len, model_width = hidden_in.shape
    cache_len_dev = cache_keys.shape[1]
    span_len = slice_len * seq_count
    inputs = hidden_in.astype(jnp.float32)
    normed = (
        inputs * lax.rsqrt(jnp.mean(inputs * inputs, axis=-1, keepdims=True) + EPSILON) * norm_gain
    ).astype(jnp.bfloat16)
    flat_rows = normed.reshape(req_local * slice_len, model_width)
    full_query, full_key, full_value = (
        lax.all_gather(w_query, ("req", "seq"), axis=0, tiled=True),
        lax.all_gather(w_key, ("req", "seq"), axis=0, tiled=True),
        lax.all_gather(w_value, ("req", "seq"), axis=0, tiled=True),
    )
    query_raw = jnp.dot(flat_rows, full_query, preferred_element_type=jnp.float32)
    key_raw = jnp.dot(flat_rows, full_key, preferred_element_type=jnp.float32)
    value_raw = jnp.dot(flat_rows, full_value, preferred_element_type=jnp.float32)
    local_index = jnp.arange(slice_len, dtype=jnp.int32)
    positions = cache_lengths[:, None] + seq_seat * slice_len + local_index[None, :]
    cosine, sine_part = tables(positions, HEAD)
    queries = (
        rotate(query_raw.reshape(req_local, slice_len, HEADS, HEAD), cosine, sine_part)
        .reshape(req_local, slice_len, HEADS * HEAD)
        .astype(jnp.bfloat16)
    )
    new_keys = (
        rotate(key_raw.reshape(req_local, slice_len, KV_HEADS, HEAD), cosine, sine_part)
        .reshape(req_local, slice_len, KV_HEADS * HEAD)
        .astype(jnp.bfloat16)
    )
    new_values = value_raw.reshape(req_local, slice_len, KV_HEADS * HEAD).astype(jnp.bfloat16)
    all_queries = lax.all_gather(queries, "seq", axis=1, tiled=True)
    key_block = jnp.concatenate([cache_keys, new_keys], axis=1)
    value_block = jnp.concatenate([cache_values, new_values], axis=1)
    span_index = jnp.arange(span_len, dtype=jnp.int32)
    cache_pos = seq_seat * cache_len_dev + jnp.arange(cache_len_dev, dtype=jnp.int32)
    new_pos = seq_seat * slice_len + local_index
    new_live = new_pos[None, :] <= span_index[:, None]
    max_list = []
    sum_list = []
    out_list = []
    for request in range(req_local):
        cache_live = cache_pos < cache_lengths[request]
        live_full = jnp.concatenate(
            [jnp.broadcast_to(cache_live[None, :], (span_len, cache_len_dev)), new_live], axis=1
        )
        query_rows = all_queries[request]
        terms = attend_rows(query_rows, key_block[request], value_block[request], live_full)
        max_list.append(terms[0])
        sum_list.append(terms[1])
        out_list.append(terms[2])
    max_all = jnp.stack(max_list)
    sum_all = jnp.stack(sum_list)
    out_all = jnp.stack(out_list)
    got_max, got_sum = (
        lax.all_to_all(max_all, "seq", split_axis=1, concat_axis=0, tiled=True),
        lax.all_to_all(sum_all, "seq", split_axis=1, concat_axis=0, tiled=True),
    )
    got_out = lax.all_to_all(out_all, "seq", split_axis=1, concat_axis=0, tiled=True)
    got_max = got_max.reshape(seq_count, req_local, slice_len, HEADS)
    got_sum = got_sum.reshape(seq_count, req_local, slice_len, HEADS)
    got_out = got_out.reshape(seq_count, req_local, slice_len, HEADS, HEAD)
    best_max = jnp.max(got_max, axis=0)
    factor = jnp.exp(got_max - best_max)
    total_sum = jnp.sum(got_sum * factor, axis=0)
    total_out = jnp.sum(got_out.astype(jnp.float32) * factor[..., None], axis=0)
    attended = (
        (total_out / total_sum[..., None])
        .reshape(req_local, slice_len, HEADS * HEAD)
        .astype(jnp.bfloat16)
    )
    return (attended, new_keys, new_values)


def solution(mesh):
    in_specs = (
        P("req", "seq", None),
        P(),
        P(("req", "seq"), None),
        P(("req", "seq"), None),
        P(("req", "seq"), None),
        P("req", "seq", None),
        P("req", "seq", None),
        P("req"),
    )
    out_specs = (P("req", "seq", None), P("req", "seq", None), P("req", "seq", None))
    return jax.shard_map(body, mesh=mesh, in_specs=in_specs, out_specs=out_specs, check_vma=False)
```

profile of v0, /device:TPU:32, one launch (start us, length us, event | category | flops | bytes accessed | tf_op | source)
XLA Modules:
  0.0 553.0 jit_solution(8246084704090221894)
XLA Ops:
  11.5 117.5 %all-gather.9.cloned.1.call-done = bf16[2048,1024]{1,0:T(8,128)(2,1)} async-done(((bf16[8,1024]{1,0:T(8,128)(2,1)}), bf16[2048,1024]{1,0:T(8,128)(2,1)}) %all-gather.9.cloned.1.call-update) | async-done | bytes 4194320 | tf_op jit(solution)/shard_map/all_gather | solution.py:91
  129.0 6.6 %copy.99 = bf16[1024,2048]{1,0:T(8,128)(2,1)} copy(bf16[1024,2048]{0,1:T(8,128)(2,1)} %bitcast.163) | data formatting | bytes 8388608 | tf_op jit(solution)/shard_map/dot_general | solution.py:95
  135.6 3.6 fusion.47
  143.7 91.3 %all-gather.7.cloned.1.call-done = bf16[2048,512]{1,0:T(8,128)(2,1)} async-done(((bf16[8,512]{1,0:T(8,128)(2,1)}), bf16[2048,512]{1,0:T(8,128)(2,1)}) %all-gather.7.cloned.1.call-update) | async-done | bytes 2097168 | tf_op jit(solution)/shard_map/all_gather | solution.py:92
  235.0 2.9 copy.97
  239.7 102.3 %all-gather.5.cloned.1.call-done = bf16[2048,512]{1,0:T(8,128)(2,1)} async-done(((bf16[8,512]{1,0:T(8,128)(2,1)}), bf16[2048,512]{1,0:T(8,128)(2,1)}) %all-gather.5.cloned.1.call-update) | async-done | bytes 2097168 | tf_op jit(solution)/shard_map/all_gather | solution.py:93
  342.0 2.1 fusion.40
  346.5 48.8 %all-gather.11.cloned.1.call-done = bf16[2,1024,1024]{2,1,0:T(8,128)(2,1)} async-done(((bf16[2,32,1024]{2,1,0:T(8,128)(2,1)}), bf16[2,1024,1024]{2,1,0:T(8,128)(2,1)}) %all-gather.11.cloned.1.call-update) | async-done | bytes 4194320 | tf_op jit(solution)/shard_map/all_gather | solution.py:112
  395.3 3.9 fusion.87
  399.1 2.3 copy.101
  401.4 3.3 fusion.4
  405.3 3.0 fusion.8
  408.4 3.1 convolution_convert_fusion.3
  412.8 3.4 fusion.5
  416.7 3.9 convolution_convert_fusion.2
  423.1 2.5 fusion.6
  426.9 2.2 fusion.12
  429.1 2.1 convolution_convert_fusion.1
  432.0 2.2 fusion.7
  435.4 3.1 convolution_convert_fusion
  445.7 2.1 reshape.179
  447.8 5.2 all-to-all-start.1
  454.9 3.1 maximum_bitcast_fusion.1
  459.2 3.3 reshape.181
  462.6 7.4 %all-to-all-start.2 = ((f32[32,1,256]{2,1,0:T(1,128)}), f32[32,1,256]{2,1,0:T(1,128)S(1)}, u32[]{:S(2)}, u32[]{:S(2)}) async-start(f32[32,1,256]{2,1,0:T(1,128)} %reshape.181), calls=%async_computation.2 | async-start | bytes 65536 | tf_op jit(solution)/shard_map/all_to_all | solution.py:137
  470.0 2.0 pad_maximum_fusion
  471.9 6.3 %copy.121 = bf16[2,1024,1024]{2,0,1:T(2,128)(2,1)} copy(bf16[2,1024,1024]{2,1,0:T(8,128)(2,1)S(1)} %pad_maximum_fusion) | data formatting | bytes 8388608 | tf_op jit(solution)/shard_map/stack | solution.py:134
  478.2 7.7 %all-to-all-start = ((bf16[2,1024,1024]{2,0,1:T(2,128)(2,1)}), bf16[2,1024,1024]{2,0,1:T(2,128)(2,1)}, u32[]{:S(2)}, u32[]{:S(2)}) async-start(bf16[2,1024,1024]{2,0,1:T(2,128)(2,1)} %copy.121), calls=%async_computation | async-start | bytes 8388608 | tf_op jit(solution)/shard_map/all_to_all | solution.py:139
  493.3 4.5 mul.173
  497.9 10.8 %mul.174 = f32[32,2,32,1024]{3,2,0,1:T(8,128)} reshape(f32[32,2,32,4,256]{4,3,2,0,1:T(4,128)} %mul.173) | data formatting | bytes 16777216 | tf_op jit(solution)/shard_map/mul | solution.py:146
  509.0 30.7 %all-to-all-done = bf16[2,1024,1024]{2,0,1:T(2,128)(2,1)} async-done(((bf16[2,1024,1024]{2,0,1:T(2,128)(2,1)}), bf16[2,1024,1024]{2,0,1:T(2,128)(2,1)}, u32[]{:S(2)}, u32[]{:S(2)}) %all-to-all-start) | async-done | bytes 4194336 | tf_op jit(solution)/shard_map/all_to_all | solution.py:139
  539.7 3.7 copy.122
  (136 shorter events, 42.0 us)
Async XLA Ops:
  7.2 121.8 %all-gather.9.cloned.1.call-start = ((), (), s32[]{:S(2)}) async-start(), calls=%async_computation.5 | async-start | bytes 4210688 | tf_op jit(solution)/shard_map/all_gather | solution.py:91
  7.9 227.1 %all-gather.7.cloned.1.call-start = ((), (), s32[]{:S(2)}) async-start(), calls=%async_computation.4 | async-start | bytes 2105344 | tf_op jit(solution)/shard_map/all_gather | solution.py:92
  8.6 333.3 %all-gather.5.cloned.1.call-start = ((), (), s32[]{:S(2)}) async-start(), calls=%async_computation.3 | async-start | bytes 2105344 | tf_op jit(solution)/shard_map/all_gather | solution.py:93
  9.4 385.9 %all-gather.11.cloned.1.call-start = ((), (), s32[]{:S(2)}) async-start(), calls=%async_computation.6 | async-start | bytes 4325376 | tf_op jit(solution)/shard_map/all_gather | solution.py:112
  129.0 6.6 %copy-start.1 = (bf16[2,32,2048]{2,1,0:T(8,128)(2,1)S(1)}, bf16[2,32,2048]{2,1,0:T(8,128)(2,1)}, u32[]{:S(2)}) copy-start(bf16[2,32,2048]{2,1,0:T(8,128)(2,1)} %param.8) | copy-start | bytes 786436
  129.0 6.6 %copy-start.16 = (f32[2048]{0:T(1024)S(1)}, f32[2048]{0:T(1024)}, u32[]{:S(2)}) copy-start(f32[2048]{0:T(1024)} %param.9) | copy-start | bytes 24580
  135.6 4.4 copy-start.27
  135.6 6.4 %copy-start.10 = (bf16[2,256,512]{2,1,0:T(8,128)(2,1)S(1)}, bf16[2,256,512]{2,1,0:T(8,128)(2,1)}, u32[]{:S(2)}) copy-start(bf16[2,256,512]{2,1,0:T(8,128)(2,1)} %param.13) | copy-start | bytes 1572868
  238.8 105.3 %copy-start.11 = (bf16[2,256,512]{2,1,0:T(8,128)(2,1)S(1)}, bf16[2,256,512]{2,1,0:T(8,128)(2,1)}, u32[]{:S(2)}) copy-start(bf16[2,256,512]{2,1,0:T(8,128)(2,1)} %param.14) | copy-start | bytes 1572868
  344.1 55.0 %copy-start.14 = (bf16[2,32,512]{2,1,0:T(8,128)(2,1)}, bf16[2,32,512]{2,1,0:T(8,128)(2,1)S(1)}, u32[]{:S(2)}) copy-start(bf16[2,32,512]{2,1,0:T(8,128)(2,1)S(1)} %fusion.40) | copy-start | bytes 196612
  405.3 3.0 copy-start.3
  405.3 3.0 copy-start.9
  412.8 4.0 copy-start.13
  416.7 3.9 copy-start.2
  426.9 2.2 copy-start.8
  426.9 2.2 copy-start.12
  426.9 2.2 copy-start.22
  435.4 3.1 copy-start.21
  439.7 2.7 copy-start.6
  441.0 2.7 copy-start.7
  442.4 2.7 copy-start.23
  442.4 2.7 copy-start.24
  442.4 2.7 copy-start.25
  442.4 2.7 copy-start.26
  443.7 9.3 %copy-start.17 = (f32[512,2,2]{0,2,1:T(2,128)S(1)}, f32[512,2,2]{0,2,1:T(2,128)}, u32[]{:S(2)}) copy-start(f32[512,2,2]{0,2,1:T(2,128)} %fusion.8) | copy-start | bytes 24580
  443.7 9.4 %copy-start.18 = (f32[512,2,2]{0,2,1:T(2,128)S(1)}, f32[512,2,2]{0,2,1:T(2,128)}, u32[]{:S(2)}) copy-start(f32[512,2,2]{0,2,1:T(2,128)} %fusion.10) | copy-start | bytes 24580
  443.7 9.4 %copy-start.19 = (f32[512,2,2]{0,2,1:T(2,128)S(1)}, f32[512,2,2]{0,2,1:T(2,128)}, u32[]{:S(2)}) copy-start(f32[512,2,2]{0,2,1:T(2,128)} %fusion.12) | copy-start | bytes 24580
  443.7 9.4 %copy-start.20 = (f32[512,2,2]{0,2,1:T(2,128)S(1)}, f32[512,2,2]{0,2,1:T(2,128)}, u32[]{:S(2)}) copy-start(f32[512,2,2]{0,2,1:T(2,128)} %fusion.14) | copy-start | bytes 24580
  447.8 14.8 %all-to-all-start.1 = ((f32[32,1,256]{2,1,0:T(1,128)}), f32[32,1,256]{2,1,0:T(1,128)S(1)}, u32[]{:S(2)}, u32[]{:S(2)}) async-start(f32[32,1,256]{2,1,0:T(1,128)} %reshape.179), calls=%async_computation.1 | async-start | bytes 65536 | tf_op jit(solution)/shard_map/all_to_all | solution.py:136
  462.6 15.7 %all-to-all-start.2 = ((f32[32,1,256]{2,1,0:T(1,128)}), f32[32,1,256]{2,1,0:T(1,128)S(1)}, u32[]{:S(2)}, u32[]{:S(2)}) async-start(f32[32,1,256]{2,1,0:T(1,128)} %reshape.181), calls=%async_computation.2 | async-start | bytes 65536 | tf_op jit(solution)/shard_map/all_to_all | solution.py:137
  478.2 61.5 %all-to-all-start = ((bf16[2,1024,1024]{2,0,1:T(2,128)(2,1)}), bf16[2,1024,1024]{2,0,1:T(2,128)(2,1)}, u32[]{:S(2)}, u32[]{:S(2)}) async-start(bf16[2,1024,1024]{2,0,1:T(2,128)(2,1)} %copy.121), calls=%async_computation | async-start | bytes 8388608 | tf_op jit(solution)/shard_map/all_to_all | solution.py:139
  539.7 4.6 copy-start
  (3 other events, 3.4 us)
Sparse Core Ops, SparseCore 0:
  11.6 117.4 all-gather.8
  132.7 102.2 all-gather.6
  238.8 103.1 all-gather.4
  345.0 50.2 all-gather.10
where the time goes:
time: 554 us; the launch traced here: 553 us
  waiting for transfers between devices  393 us (71%)
  local copies, waits for them, and re-layouts  73.6 us (13%)
  matrix products  30 us (5%)
  other arithmetic  22 us (4%)
  starting transfers between devices  20.5 us (4%)
  between operations  14.2 us (3%)
    all_gather x1, waiting for transfers between devices, body(): lax.all_gather(w_query, ('req', 'seq'), axis=0, tiled=True)  118 us
    all_gather x1, waiting for transfers between devices, body(): lax.all_gather(w_value, ('req', 'seq'), axis=0, tiled=True)  102 us
    all_gather x1, waiting for transfers between devices, body(): lax.all_gather(w_key, ('req', 'seq'), axis=0, tiled=True)  91.3 us
    all_gather x1, waiting for transfers between devices, body(): all_queries = lax.all_gather(queries, 'seq', axis=1, tiled=True)  48.8 us
    all_to_all x1, waiting for transfers between devices, body(): lax.all_to_all(out_all, 'seq', split_axis=1, concat_axis=0, tiled=True)  30.7 us
    mul x2, local copies, waits for them, and re-layouts, body(): total_out = jnp.sum(got_out.astype(jnp.float32) * factor[..., None], axis=0)  15.3 us
    dot_general x4, matrix products, attend(): jnp.einsum('cgek,kgh->cgeh', weights.astype(jnp.bfloat16), value_view, pr...  12.1 us
    dot_general x4, matrix products, attend(): jnp.einsum('cgeh,kgh->cgek', query_view, key_view, preferred_element_type...  11.4 us
  transfers between devices with their start and end apart: 7, of which 5 were waited for; matrix products, arithmetic and copies ran while one was open for 12% of the time, Pallas kernels for 0%

commit v1 on v0

--- a/solution.py
+++ b/solution.py
@@ -87,14 +87,22 @@
         inputs * lax.rsqrt(jnp.mean(inputs * inputs, axis=-1, keepdims=True) + EPSILON) * norm_gain
     ).astype(jnp.bfloat16)
     flat_rows = normed.reshape(req_local * slice_len, model_width)
-    full_query, full_key, full_value = (
-        lax.all_gather(w_query, ("req", "seq"), axis=0, tiled=True),
-        lax.all_gather(w_key, ("req", "seq"), axis=0, tiled=True),
-        lax.all_gather(w_value, ("req", "seq"), axis=0, tiled=True),
+    req_count = lax.axis_size("req")
+    row_local = w_query.shape[0]
+    query_cols = w_query.shape[1]
+    key_cols = w_key.shape[1]
+    joined = jnp.concatenate([w_query, w_key, w_value], axis=1)
+    joined = lax.all_gather(joined, "req", axis=0, tiled=True)
+    joined = lax.all_gather(joined, "seq", axis=0, tiled=True)
+    permuted_rows = (
+        flat_rows.reshape(-1, req_count, seq_count, row_local)
+        .transpose(0, 2, 1, 3)
+        .reshape(-1, model_width)
     )
-    query_raw = jnp.dot(flat_rows, full_query, preferred_element_type=jnp.float32)
-    key_raw = jnp.dot(flat_rows, full_key, preferred_element_type=jnp.float32)
-    value_raw = jnp.dot(flat_rows, full_value, preferred_element_type=jnp.float32)
+    projected = jnp.dot(permuted_rows, joined, preferred_element_type=jnp.float32)
+    query_raw = projected[:, :query_cols]
+    key_raw = projected[:, query_cols : query_cols + key_cols]
+    value_raw = projected[:, query_cols + key_cols :]
     local_index = jnp.arange(slice_len, dtype=jnp.int32)
     positions = cache_lengths[:, None] + seq_seat * slice_len + local_index[None, :]
     cosine, sine_part = tables(positions, HEAD)

time: 554 us -> 330 us (0.60)
  waiting for transfers between devices: 393 us -> 129 us
  blocking collectives: 0 us -> 29.7 us
  local copies, waits for them, and re-layouts: 73.6 us -> 82.3 us
    all_gather x3 -> x1, waiting for transfers between devices: 311 us -> 53.9 us  [body(): joined = lax.all_gather(joined, 'seq', axis=0, tiled=True)]
    all_gather x0 -> x1, blocking collectives: none -> 29.7 us  [body(): joined = lax.all_gather(joined, 'req', axis=0, tiled=True)]
    unnamed x61 -> x57, local copies, waits for them, and re-layouts: 9.83 us -> 26.2 us
    dot_general x2 -> x0, local copies, waits for them, and re-layouts: 9.51 us -> none  [the longest x1 6.59 us: body(): jnp.dot(flat_rows, full_query, preferred_element_type=jnp.float32)]
  transfers between devices with their start and end apart: 7 -> 5, of which waited for: 5 -> 3; matrix products, arithmetic and copies ran while one was open for 12% -> 16% of each run, Pallas kernels for 0% -> 0%
where the time goes in v1:
time: 330 us; the launch traced here: 329 us
  waiting for transfers between devices  129 us (39%)
  local copies, waits for them, and re-layouts  82.3 us (25%)
  blocking collectives  29.7 us (9%)
  matrix products  29.2 us (9%)
  other arithmetic  24.2 us (7%)
  starting transfers between devices  20.5 us (6%)
  between operations  14.6 us (4%)
    all_gather x1, waiting for transfers between devices, body(): joined = lax.all_gather(joined, 'seq', axis=0, tiled=True)  53.9 us
    all_gather x1, waiting for transfers between devices, body(): all_queries = lax.all_gather(queries, 'seq', axis=1, tiled=True)  44.1 us
    all_to_all x1, waiting for transfers between devices, body(): lax.all_to_all(out_all, 'seq', split_axis=1, concat_axis=0, tiled=True)  30.7 us
    all_gather x1, blocking collectives, body(): joined = lax.all_gather(joined, 'req', axis=0, tiled=True)  29.7 us
    unnamed x57, local copies, waits for them, and re-layouts  26.2 us
    mul x2, local copies, waits for them, and re-layouts, body(): total_out = jnp.sum(got_out.astype(jnp.float32) * factor[..., None], axis=0)  15.3 us
    dot_general x4, matrix products, attend(): jnp.einsum('cgek,kgh->cgeh', weights.astype(jnp.bfloat16), value_view, pr...  13 us
    dot_general x4, matrix products, attend(): jnp.einsum('cgeh,kgh->cgek', query_view, key_view, preferred_element_type...  11.1 us
  transfers between devices with their start and end apart: 5, of which 3 were waited for; matrix products, arithmetic and copies ran while one was open for 16% of the time, Pallas kernels for 0%

profile of v1, /device:TPU:32, one launch (start us, length us, event | category | flops | bytes accessed | tf_op | source)
XLA Modules:
  0.0 329.1 jit_solution(13807412647260015121)
XLA Ops:
  8.0 29.7 %all_gather.9 = bf16[64,2048]{1,0:T(8,128)(2,1)} all-gather(bf16[8,2048]{1,0:T(8,128)(2,1)S(1)} %pad_maximum_fusion.4), channel_id=1, replica_groups=mesh['req'=8,'seq'=32] {'req'}, dimensions={0}, use_global_device_ids=true | all-gather | bytes 294912 | tf_op jit(solution)/shard_map/all_gather | solution.py:95
  41.6 53.9 %all-gather.3.cloned.1.call-done = bf16[2048,2048]{1,0:T(8,128)(2,1)} async-done(((bf16[64,2048]{1,0:T(8,128)(2,1)}), bf16[2048,2048]{1,0:T(8,128)(2,1)}) %all-gather.3.cloned.1.call-update) | async-done | bytes 8388624 | tf_op jit(solution)/shard_map/all_gather | solution.py:96
  95.5 5.0 %fusion.80 = f32[64,2048]{1,0:T(8,128)S(1)} fusion(bf16[64,2048]{0,1:T(8,128)(2,1)S(1)} %bitcast.144, bf16[2048,2048]{1,0:T(8,128)(2,1)} %all-gather.3.cloned.1.call-done), kind=kOutput, calls=%fused_computation.127 | convolution fusion | flops 536870912 | bytes 9175040 | tf_op jit(solution)/shard_map/dot_general | solution.py:102
  108.4 44.1 %all-gather.5.cloned.1.call-done = bf16[2,1024,1024]{2,0,1:T(2,128)(2,1)} async-done(((bf16[2,32,1024]{2,0,1:T(2,128)(2,1)}), bf16[2,1024,1024]{2,0,1:T(2,128)(2,1)}) %all-gather.5.cloned.1.call-update) | async-done | bytes 4194320 | tf_op jit(solution)/shard_map/all_gather | solution.py:120
  152.5 10.8 %fusion.75 = (bf16[1,512,1024]{2,0,1:T(2,128)(2,1)}, bf16[1,512,1024]{2,0,1:T(2,128)(2,1)}, bf16[1,512,1024]{2,0,1:T(2,128)(2,1)}, bf16[1,512,1024]{2,0,1:T(2,128)(2,1)S(1)}) fusion(bf16[2,1024,1024]{2,0,1:T(2,128)(2,1)} %all-gather.5.cloned.1.call-done), kind=kLoop, calls=%fused_computation.122 | loop fusion | bytes 8388608 | tf_op jit(solution)/shard_map/slice | solution.py:70
  163.3 4.6 %copy.144 = bf16[1,512,1024]{1,2,0:T(8,128)(2,1)S(1)} copy(bf16[1,512,1024]{2,0,1:T(2,128)(2,1)} %get-tuple-element.3) | data formatting | bytes 2097152
  167.9 3.0 fusion.2
  171.5 3.0 fusion.6
  174.5 3.0 convolution_convert_fusion.3
  177.5 4.6 %copy.145 = bf16[1,512,1024]{1,2,0:T(8,128)(2,1)S(1)} copy(bf16[1,512,1024]{2,0,1:T(2,128)(2,1)} %get-tuple-element.5) | data formatting | bytes 2097152
  182.1 3.0 fusion.3
  185.7 3.9 %convolution_convert_fusion.2 = bf16[2,256,512,2]{2,1,3,0:T(8,128)(2,1)} fusion(f32[2,288,512,2]{2,1,3,0:T(8,128)} %get-tuple-element.30, f32[512,2,2]{0,2,1:T(2,128)S(1)} %get-tuple-element.29, pred[512,288]{0,1:T(8,128)(4,1)} %get-tuple-element.14, bf16[288,2,256,1]{2,1,0,3:T(2,128)(2,1)} %bitcast.161), kind=kOutput, calls=%fused_computation.28 | convolution fusion | flops 305463296 | bytes 3858432 | tf_op jit(solution)/shard_map/cgek,kgh->cgeh/dot_general | solution.py:50
  190.9 4.7 %copy.146 = bf16[1,512,1024]{1,2,0:T(8,128)(2,1)S(1)} copy(bf16[1,512,1024]{2,0,1:T(2,128)(2,1)} %get-tuple-element.4) | data formatting | bytes 2097152
  195.6 3.0 fusion.4
  199.2 3.0 fusion.10
  202.2 3.0 convolution_convert_fusion.1
  205.2 2.6 copy.147
  207.8 2.2 fusion.5
  211.3 3.0 convolution_convert_fusion
  221.5 2.1 reshape.178
  223.6 5.3 %all-to-all-start.1 = ((f32[32,1,256]{2,1,0:T(1,128)}), f32[32,1,256]{2,1,0:T(1,128)S(1)}, u32[]{:S(2)}, u32[]{:S(2)}) async-start(f32[32,1,256]{2,1,0:T(1,128)} %reshape.178), calls=%async_computation.1 | async-start | bytes 65536 | tf_op jit(solution)/shard_map/all_to_all | solution.py:144
  229.0 1.7 maximum_bitcast_fusion
  230.7 3.0 maximum_bitcast_fusion.1
  235.0 3.3 %reshape.180 = f32[32,1,256]{2,1,0:T(1,128)} reshape(f32[1024,2,4]{2,1,0:T(2,128)} %bitcast.141) | data formatting | bytes 65536
  238.4 7.6 %all-to-all-start.2 = ((f32[32,1,256]{2,1,0:T(1,128)}), f32[32,1,256]{2,1,0:T(1,128)S(1)}, u32[]{:S(2)}, u32[]{:S(2)}) async-start(f32[32,1,256]{2,1,0:T(1,128)} %reshape.180), calls=%async_computation.2 | async-start | bytes 65536 | tf_op jit(solution)/shard_map/all_to_all | solution.py:145
  246.0 2.0 pad_maximum_fusion
  248.0 6.3 %copy.107 = bf16[2,1024,1024]{2,0,1:T(2,128)(2,1)} copy(bf16[2,1024,1024]{2,1,0:T(8,128)(2,1)S(1)} %pad_maximum_fusion) | data formatting | bytes 8388608 | tf_op jit(solution)/shard_map/stack | solution.py:142
  254.3 7.6 %all-to-all-start = ((bf16[2,1024,1024]{2,0,1:T(2,128)(2,1)}), bf16[2,1024,1024]{2,0,1:T(2,128)(2,1)}, u32[]{:S(2)}, u32[]{:S(2)}) async-start(bf16[2,1024,1024]{2,0,1:T(2,128)(2,1)} %copy.107), calls=%async_computation | async-start | bytes 8388608 | tf_op jit(solution)/shard_map/all_to_all | solution.py:147
  269.2 4.5 %mul.173 = f32[32,2,32,4,256]{4,3,2,0,1:T(4,128)} broadcast(f32[32,2,32,4]{3,2,0,1:T(8,128)S(1)} %copy.111), dimensions={0,1,2,3} | broadcast | bytes 8421376 | tf_op jit(solution)/shard_map/mul | solution.py:154
  273.7 10.8 %mul.174 = f32[32,2,32,1024]{3,2,0,1:T(8,128)} reshape(f32[32,2,32,4,256]{4,3,2,0,1:T(4,128)} %mul.173) | data formatting | bytes 16777216 | tf_op jit(solution)/shard_map/mul | solution.py:154
  284.8 30.7 %all-to-all-done = bf16[2,1024,1024]{2,0,1:T(2,128)(2,1)} async-done(((bf16[2,1024,1024]{2,0,1:T(2,128)(2,1)}), bf16[2,1024,1024]{2,0,1:T(2,128)(2,1)}, u32[]{:S(2)}, u32[]{:S(2)}) %all-to-all-start) | async-done | bytes 4194336 | tf_op jit(solution)/shard_map/all_to_all | solution.py:147
  315.5 3.7 %copy.108 = bf16[2,1024,1024]{2,1,0:T(8,128)(2,1)S(1)} copy(bf16[2,1024,1024]{2,0,1:T(2,128)(2,1)} %all-to-all-done) | data formatting | bytes 8388608 | tf_op jit(solution)/shard_map/all_to_all | solution.py:147
  (130 shorter events, 35.9 us)
Async XLA Ops:
  7.2 88.3 %all-gather.3.cloned.1.call-start = ((), (), s32[]{:S(2)}) async-start(), calls=%async_computation.3 | async-start | bytes 8650752 | tf_op jit(solution)/shard_map/all_gather | solution.py:96
  37.6 114.9 %all-gather.5.cloned.1.call-start = ((), (), s32[]{:S(2)}) async-start(), calls=%async_computation.4 | async-start | bytes 4325376 | tf_op jit(solution)/shard_map/all_gather | solution.py:120
  37.7 3.6 %copy-start.23 = (s32[2]{0:T(128)S(1)}, s32[2]{0:T(128)}, u32[]{:S(2)}) copy-start(s32[2]{0:T(128)} %param.15) | copy-start | bytes 28
  100.4 3.1 copy-start.10
  103.7 2.2 copy-start.11
  104.8 2.8 copy-start.12
  105.1 3.3 %copy-start.13 = (bf16[2,32,512]{2,1,0:T(8,128)(2,1)}, bf16[2,32,512]{2,1,0:T(8,128)(2,1)S(1)}, u32[]{:S(2)}) copy-start(bf16[2,32,512]{2,1,0:T(8,128)(2,1)S(1)} %convert_element_type.90) | copy-start | bytes 196612
  170.9 3.6 %copy-start.9 = (pred[512,288]{0,1:T(8,128)(4,1)S(1)}, pred[512,288]{0,1:T(8,128)(4,1)}, u32[]{:S(2)}) copy-start(pred[512,288]{0,1:T(8,128)(4,1)} %get-tuple-element.13) | copy-start | bytes 442372
  171.5 3.0 copy-start.2
  185.7 3.9 %copy-start.1 = (f32[2,288,512,2]{2,1,3,0:T(8,128)S(1)}, f32[2,288,512,2]{2,1,3,0:T(8,128)}, u32[]{:S(2)}) copy-start(f32[2,288,512,2]{2,1,3,0:T(8,128)} %get-tuple-element.30) | copy-start | bytes 7077892
  185.7 3.9 %copy-start.8 = (pred[512,288]{0,1:T(8,128)(4,1)S(1)}, pred[512,288]{0,1:T(8,128)(4,1)}, u32[]{:S(2)}) copy-start(pred[512,288]{0,1:T(8,128)(4,1)} %get-tuple-element.14) | copy-start | bytes 442372
  199.2 3.0 copy-start.3
  211.3 3.1 copy-start.18
  214.3 1.2 copy-start.4
  215.5 1.3 copy-start.5
  215.5 2.6 copy-start.6
  216.9 2.7 copy-start.7
  218.2 2.7 copy-start.19
  218.2 2.7 copy-start.20
  218.2 2.7 copy-start.21
  218.2 2.7 copy-start.22
  219.5 9.3 %copy-start.14 = (f32[512,2,2]{0,2,1:T(2,128)S(1)}, f32[512,2,2]{0,2,1:T(2,128)}, u32[]{:S(2)}) copy-start(f32[512,2,2]{0,2,1:T(2,128)} %fusion.6) | copy-start | bytes 24580
  219.5 9.4 %copy-start.15 = (f32[512,2,2]{0,2,1:T(2,128)S(1)}, f32[512,2,2]{0,2,1:T(2,128)}, u32[]{:S(2)}) copy-start(f32[512,2,2]{0,2,1:T(2,128)} %fusion.8) | copy-start | bytes 24580
  219.5 9.4 %copy-start.16 = (f32[512,2,2]{0,2,1:T(2,128)S(1)}, f32[512,2,2]{0,2,1:T(2,128)}, u32[]{:S(2)}) copy-start(f32[512,2,2]{0,2,1:T(2,128)} %fusion.10) | copy-start | bytes 24580
  219.5 9.4 %copy-start.17 = (f32[512,2,2]{0,2,1:T(2,128)S(1)}, f32[512,2,2]{0,2,1:T(2,128)}, u32[]{:S(2)}) copy-start(f32[512,2,2]{0,2,1:T(2,128)} %fusion.12) | copy-start | bytes 24580
  223.6 14.8 %all-to-all-start.1 = ((f32[32,1,256]{2,1,0:T(1,128)}), f32[32,1,256]{2,1,0:T(1,128)S(1)}, u32[]{:S(2)}, u32[]{:S(2)}) async-start(f32[32,1,256]{2,1,0:T(1,128)} %reshape.178), calls=%async_computation.1 | async-start | bytes 65536 | tf_op jit(solution)/shard_map/all_to_all | solution.py:144
  238.4 15.9 %all-to-all-start.2 = ((f32[32,1,256]{2,1,0:T(1,128)}), f32[32,1,256]{2,1,0:T(1,128)S(1)}, u32[]{:S(2)}, u32[]{:S(2)}) async-start(f32[32,1,256]{2,1,0:T(1,128)} %reshape.180), calls=%async_computation.2 | async-start | bytes 65536 | tf_op jit(solution)/shard_map/all_to_all | solution.py:145
  254.3 61.3 %all-to-all-start = ((bf16[2,1024,1024]{2,0,1:T(2,128)(2,1)}), bf16[2,1024,1024]{2,0,1:T(2,128)(2,1)}, u32[]{:S(2)}, u32[]{:S(2)}) async-start(bf16[2,1024,1024]{2,0,1:T(2,128)(2,1)} %copy.107), calls=%async_computation | async-start | bytes 8388608 | tf_op jit(solution)/shard_map/all_to_all | solution.py:147
  315.5 4.6 %copy-start = (f32[32,2,32,1024]{3,2,0,1:T(8,128)S(1)}, f32[32,2,32,1024]{3,2,0,1:T(8,128)}, u32[]{:S(2)}) copy-start(f32[32,2,32,1024]{3,2,0,1:T(8,128)} %mul.174) | copy-start | bytes 25165828
Sparse Core Ops, SparseCore 0:
  37.8 57.6 all-gather.2
  101.8 50.6 all-gather.4

commit v2 on v1

--- a/solution.py
+++ b/solution.py
@@ -1,6 +1,10 @@
+import functools
+
 import jax
 import jax.numpy as jnp
 from jax import lax
+from jax.experimental import pallas as pl
+from jax.experimental.pallas import tpu as pltpu
 from jax.sharding import PartitionSpec as P
 
 HEADS = 4
@@ -74,6 +78,70 @@
             )
         )
     return tuple((jnp.concatenate([piece[slot] for piece in pieces], axis=0) for slot in range(3)))
+
+
+def attention_kernel(scalar_ref, query_ref, key_ref, value_ref, stats_ref, out_ref, *, cache_len_dev, slice_len):
+    request = pl.program_id(0)
+    length = scalar_ref[request]
+    seat = scalar_ref[scalar_ref.shape[0] - 1]
+    span_len = query_ref.shape[1]
+    key_rows = key_ref.shape[1]
+    key_index = lax.broadcasted_iota(jnp.int32, (span_len, key_rows), 1)
+    query_index = lax.broadcasted_iota(jnp.int32, (span_len, key_rows), 0)
+    cache_live = seat * cache_len_dev + key_index < length
+    new_live = seat * slice_len + (key_index - cache_len_dev) <= query_index
+    in_cache = key_index < cache_len_dev
+    in_new = jnp.logical_not(in_cache) & (key_index < cache_len_dev + slice_len)
+    live = (in_cache & cache_live) | (in_new & new_live)
+    lane = lax.broadcasted_iota(jnp.int32, (span_len, 128), 1)
+    stats = jnp.zeros((span_len, 128), jnp.float32)
+    group_size = HEADS // KV_HEADS
+    for head in range(HEADS):
+        group = head // group_size
+        query_rows = query_ref[0, :, head * HEAD : (head + 1) * HEAD]
+        key_rows_h = key_ref[0, :, group * HEAD : (group + 1) * HEAD]
+        value_rows_h = value_ref[0, :, group * HEAD : (group + 1) * HEAD]
+        scores = lax.dot_general(
+            query_rows, key_rows_h, (((1,), (1,)), ((), ())), preferred_element_type=jnp.float32
+        ) * HEAD ** (-0.5)
+        scores = jnp.where(live, scores, MASKED)
+        block_max = jnp.max(scores, axis=1, keepdims=True)
+        weights = jnp.where(live, jnp.exp(scores - block_max), 0.0)
+        block_sum = jnp.sum(weights, axis=1, keepdims=True)
+        block_out = jnp.dot(
+            weights.astype(jnp.bfloat16), value_rows_h, preferred_element_type=jnp.float32
+        )
+        out_ref[0, :, head * HEAD : (head + 1) * HEAD] = block_out.astype(jnp.bfloat16)
+        stats = jnp.where(lane == head, block_max, stats)
+        stats = jnp.where(lane == HEADS + head, block_sum, stats)
+    stats_ref[0] = stats
+
+
+def block_attention(all_queries, key_block, value_block, scalars, cache_len_dev, slice_len):
+    req_local, span_len, query_width = all_queries.shape
+    key_rows = key_block.shape[1]
+    kv_width = key_block.shape[2]
+    grid_spec = pltpu.PrefetchScalarGridSpec(
+        num_scalar_prefetch=1,
+        grid=(req_local,),
+        in_specs=[
+            pl.BlockSpec((1, span_len, query_width), lambda r, s: (r, 0, 0)),
+            pl.BlockSpec((1, key_rows, kv_width), lambda r, s: (r, 0, 0)),
+            pl.BlockSpec((1, key_rows, kv_width), lambda r, s: (r, 0, 0)),
+        ],
+        out_specs=[
+            pl.BlockSpec((1, span_len, 128), lambda r, s: (r, 0, 0)),
+            pl.BlockSpec((1, span_len, query_width), lambda r, s: (r, 0, 0)),
+        ],
+    )
+    return pl.pallas_call(
+        functools.partial(attention_kernel, cache_len_dev=cache_len_dev, slice_len=slice_len),
+        grid_spec=grid_spec,
+        out_shape=[
+            jax.ShapeDtypeStruct((req_local, span_len, 128), jnp.float32),
+            jax.ShapeDtypeStruct((req_local, span_len, query_width), jnp.bfloat16),
+        ],
+    )(scalars, all_queries, key_block, value_block)
 
 
 def body(hidden_in, norm_gain, w_query, w_key, w_value, cache_keys, cache_values, cache_lengths):
@@ -118,35 +186,22 @@
     )
     new_values = value_raw.reshape(req_local, slice_len, KV_HEADS * HEAD).astype(jnp.bfloat16)
     all_queries = lax.all_gather(queries, "seq", axis=1, tiled=True)
-    key_block = jnp.concatenate([cache_keys, new_keys], axis=1)
-    value_block = jnp.concatenate([cache_values, new_values], axis=1)
-    span_index = jnp.arange(span_len, dtype=jnp.int32)
-    cache_pos = seq_seat * cache_len_dev + jnp.arange(cache_len_dev, dtype=jnp.int32)
-    new_pos = seq_seat * slice_len + local_index
-    new_live = new_pos[None, :] <= span_index[:, None]
-    max_list = []
-    sum_list = []
-    out_list = []
-    for request in range(req_local):
-        cache_live = cache_pos < cache_lengths[request]
-        live_full = jnp.concatenate(
-            [jnp.broadcast_to(cache_live[None, :], (span_len, cache_len_dev)), new_live], axis=1
-        )
-        query_rows = all_queries[request]
-        terms = attend_rows(query_rows, key_block[request], value_block[request], live_full)
-        max_list.append(terms[0])
-        sum_list.append(terms[1])
-        out_list.append(terms[2])
-    max_all = jnp.stack(max_list)
-    sum_all = jnp.stack(sum_list)
-    out_all = jnp.stack(out_list)
-    got_max, got_sum = (
-        lax.all_to_all(max_all, "seq", split_axis=1, concat_axis=0, tiled=True),
-        lax.all_to_all(sum_all, "seq", split_axis=1, concat_axis=0, tiled=True),
-    )
+    pad_rows = (-(cache_len_dev + slice_len)) % 128
+    key_block = jnp.concatenate(
+        [cache_keys, new_keys, jnp.zeros((req_local, pad_rows, KV_HEADS * HEAD), jnp.bfloat16)], axis=1
+    )
+    value_block = jnp.concatenate(
+        [cache_values, new_values, jnp.zeros((req_local, pad_rows, KV_HEADS * HEAD), jnp.bfloat16)],
+        axis=1,
+    )
+    scalars = jnp.concatenate([cache_lengths.astype(jnp.int32), seq_seat.astype(jnp.int32)[None]])
+    stats, out_all = block_attention(all_queries, key_block, value_block, scalars, cache_len_dev, slice_len)
+    stats = stats[:, :, : 2 * HEADS]
+    got_stats = lax.all_to_all(stats, "seq", split_axis=1, concat_axis=0, tiled=True)
     got_out = lax.all_to_all(out_all, "seq", split_axis=1, concat_axis=0, tiled=True)
-    got_max = got_max.reshape(seq_count, req_local, slice_len, HEADS)
-    got_sum = got_sum.reshape(seq_count, req_local, slice_len, HEADS)
+    got_stats = got_stats.reshape(seq_count, req_local, slice_len, 2 * HEADS)
+    got_max = got_stats[..., :HEADS]
+    got_sum = got_stats[..., HEADS:]
     got_out = got_out.reshape(seq_count, req_local, slice_len, HEADS, HEAD)
     best_max = jnp.max(got_max, axis=0)
     factor = jnp.exp(got_max - best_max)

time: 330 us -> 260 us (0.79)
  local copies, waits for them, and re-layouts: 82.3 us -> 34.7 us
  matrix products: 29.2 us -> 5.07 us
  Pallas kernels: 0 us -> 10.5 us
  starting transfers between devices: 20.5 us -> 12.8 us
  other arithmetic: 24.2 us -> 17.6 us
  waiting for transfers between devices: 129 us -> 135 us
    dot_general x8 -> x0, matrix products: 24.2 us -> none  [the longest x4 13 us: attend(): jnp.einsum('cgek,kgh->cgeh', weights.astype(jnp.bfloat16), value_view, pr...]
    unnamed x57 -> x13, local copies, waits for them, and re-layouts: 26.2 us -> 4.52 us
    another operation x7 -> x1, local copies, waits for them, and re-layouts: 11.3 us -> 0.01 us  [the longest x1 6.28 us: body(): out_all = jnp.stack(out_list)]
    pallas_call x0 -> x1, Pallas kernels: none -> 10.5 us  [block_attention(): pl.pallas_call(functools.partial(attention_kernel, cache_len_dev=cache_le...]
    slice x5 -> x1, local copies, waits for them, and re-layouts: 12.2 us -> 2.04 us  [body(): stats = stats[:, :, :2 * HEADS]]
    pallas_call x0 -> x1, local copies, waits for them, and re-layouts: none -> 8.44 us  [block_attention(): pl.pallas_call(functools.partial(attention_kernel, cache_len_dev=cache_le...]
    reduce_sum x1, other arithmetic: 1.34 us -> 9.3 us  [body(): total_out = jnp.sum(got_out.astype(jnp.float32) * factor[..., None], axis=0)]
    all_to_all x2 -> x1, starting transfers between devices: 12.9 us -> 5.43 us  [body(): lax.all_to_all(stats, 'seq', split_axis=1, concat_axis=0, tiled=True)]
  transfers between devices with their start and end apart: 5 -> 4, of which waited for: 3 -> 3; matrix products, arithmetic and copies ran while one was open for 16% -> 14% of each run, Pallas kernels for 0% -> 0%
where the time goes in v2:
time: 260 us; the launch traced here: 259 us
  waiting for transfers between devices  135 us (52%)
  local copies, waits for them, and re-layouts  34.7 us (13%)
  blocking collectives  29.7 us (11%)
  other arithmetic  17.6 us (7%)
  between operations  14.3 us (6%)
  starting transfers between devices  12.8 us (5%)
  Pallas kernels  10.5 us (4%)
  matrix products  5.07 us (2%)
    all_gather x1, waiting for transfers between devices, body(): joined = lax.all_gather(joined, 'seq', axis=0, tiled=True)  53.9 us
    all_gather x1, waiting for transfers between devices, body(): all_queries = lax.all_gather(queries, 'seq', axis=1, tiled=True)  48.3 us
    all_to_all x1, waiting for transfers between devices, body(): lax.all_to_all(out_all, 'seq', split_axis=1, concat_axis=0, tiled=True)  32.5 us
    all_gather x1, blocking collectives, body(): joined = lax.all_gather(joined, 'req', axis=0, tiled=True)  29.7 us
    mul x2, local copies, waits for them, and re-layouts, body(): total_out = jnp.sum(got_out.astype(jnp.float32) * factor[..., None], axis=0)  16.3 us
    pallas_call x1, Pallas kernels, block_attention(): pl.pallas_call(functools.partial(attention_kernel, cache_len_dev=cache_le...  10.5 us
    reduce_sum x1, other arithmetic, body(): total_out = jnp.sum(got_out.astype(jnp.float32) * factor[..., None], axis=0)  9.3 us
    pallas_call x1, local copies, waits for them, and re-layouts, block_attention(): pl.pallas_call(functools.partial(attention_kernel, cache_len_dev=cache_le...  8.44 us
  transfers between devices with their start and end apart: 4, of which 3 were waited for; matrix products, arithmetic and copies ran while one was open for 14% of the time, Pallas kernels for 0%

profile of v2, /device:TPU:32, one launch (start us, length us, event | category | flops | bytes accessed | tf_op | source)
XLA Modules:
  0.0 259.4 jit_solution(2793518593698987478)
XLA Ops:
  7.2 0.8 pad_maximum_fusion.2
  8.0 29.7 %all_gather.9 = bf16[64,2048]{1,0:T(8,128)(2,1)} all-gather(bf16[8,2048]{1,0:T(8,128)(2,1)S(1)} %pad_maximum_fusion.2), channel_id=1, replica_groups=mesh['req'=8,'seq'=32] {'req'}, dimensions={0}, use_global_device_ids=true | all-gather | bytes 294912 | tf_op jit(solution)/shard_map/all_gather | solution.py:163
  37.7 1.1 fusion.3
  38.8 1.1 fusion.5
  39.9 0.7 copy.17
  40.6 0.5 reshape_reshape.3
  41.1 0.1 copy.18
  41.4 0.2 multiply_cosine_fusion
  41.6 53.9 %all-gather.3.cloned.1.call-done = bf16[2048,2048]{1,0:T(8,128)(2,1)} async-done(((bf16[64,2048]{1,0:T(8,128)(2,1)}), bf16[2048,2048]{1,0:T(8,128)(2,1)}) %all-gather.3.cloned.1.call-update) | async-done | bytes 8388624 | tf_op jit(solution)/shard_map/all_gather | solution.py:164
  95.5 5.1 %fusion.6 = f32[64,2048]{1,0:T(8,128)S(1)} fusion(bf16[64,2048]{0,1:T(8,128)(2,1)S(1)} %bitcast.31, bf16[2048,2048]{1,0:T(8,128)(2,1)} %all-gather.3.cloned.1.call-done), kind=kOutput, calls=%fused_computation.31 | convolution fusion | flops 536870912 | bytes 9175040 | tf_op jit(solution)/shard_map/dot_general | solution.py:170
  100.9 0.7 convert_element_type.41
  101.7 0.6 pad_add_fusion.scalar_ref
  102.7 1.5 maximum_maximum_fusion.1
  104.1 48.3 %all-gather.5.cloned.1.call-done.query_ref = bf16[2,1024,1024]{2,1,0:T(8,128)(2,1)} async-done(((bf16[2,32,1024]{2,1,0:T(8,128)(2,1)}), bf16[2,1024,1024]{2,1,0:T(8,128)(2,1)}) %all-gather.5.cloned.1.call-update) | async-done | bytes 4194320 | tf_op jit(solution)/shard_map/all_gather | solution.py:188
  152.5 10.5 %shard_map.103 = (f32[2,1024,128]{2,1,0:T(8,128)}, bf16[2,1024,1024]{2,1,0:T(8,128)(2,1)}) custom-call(s32[3]{0:T(128)} %pad_add_fusion.scalar_ref, bf16[2,1024,1024]{2,1,0:T(8,128)(2,1)} %all-gather.5.cloned.1.call-done.query_ref, bf16[2,384,512]{2,1,0:T(8,128)(2,1)} %get-tuple-element.19.key_ref, bf16[2,384,512]{2,1,0:T(8,128)(2,1)} %get-tuple-element.18.value_ref), custom_call_target="tpu_custom_call" | custom-call | tf_op jit(solution)/shard_map/pallas_call | solution.py:137
  163.0 2.0 copy.23
  165.0 2.2 reshape.81
  167.2 5.4 %all-to-all-start.1 = ((f32[32,1,512]{2,1,0:T(1,128)}), f32[32,1,512]{2,1,0:T(1,128)S(1)}, u32[]{:S(2)}, u32[]{:S(2)}) async-start(f32[32,1,512]{2,1,0:T(1,128)} %reshape.81), calls=%async_computation.1 | async-start | bytes 131072 | tf_op jit(solution)/shard_map/all_to_all | solution.py:200
  172.7 8.4 %copy.19 = bf16[2,1024,1024]{2,0,1:T(2,128)(2,1)} copy(bf16[2,1024,1024]{2,1,0:T(8,128)(2,1)} %get-tuple-element.5) | data formatting | bytes 8388608 | tf_op jit(solution)/shard_map/pallas_call | solution.py:137
  181.1 7.3 %all-to-all-start = ((bf16[2,1024,1024]{2,0,1:T(2,128)(2,1)}), bf16[2,1024,1024]{2,0,1:T(2,128)(2,1)}, u32[]{:S(2)}, u32[]{:S(2)}) async-start(bf16[2,1024,1024]{2,0,1:T(2,128)(2,1)} %copy.19), calls=%async_computation | async-start | bytes 8388608 | tf_op jit(solution)/shard_map/all_to_all | solution.py:201
  188.4 0.5 broadcast.64
  189.0 0.8 reduce.1
  189.8 1.6 reshape.82
  191.4 0.4 slice_reduce_fusion
  191.8 1.4 fusion.2
  193.2 4.5 %mul.136 = f32[32,2,32,4,256]{4,3,1,2,0:T(4,128)} broadcast(f32[32,2,32,4]{3,1,2,0:T(2,128)S(1)} %get-tuple-element.11), dimensions={0,1,2,3} | broadcast | bytes 8421376 | tf_op jit(solution)/shard_map/mul | solution.py:209
  197.7 11.8 %mul.137 = f32[32,2,32,1024]{3,1,2,0:T(2,128)} reshape(f32[32,2,32,4,256]{4,3,1,2,0:T(4,128)} %mul.136) | data formatting | bytes 16777216 | tf_op jit(solution)/shard_map/mul | solution.py:209
  209.7 0.2 div.28
  209.9 32.5 %all-to-all-done = bf16[2,1024,1024]{2,0,1:T(2,128)(2,1)} async-done(((bf16[2,1024,1024]{2,0,1:T(2,128)(2,1)}), bf16[2,1024,1024]{2,0,1:T(2,128)(2,1)}, u32[]{:S(2)}, u32[]{:S(2)}) %all-to-all-start) | async-done | bytes 4194336 | tf_op jit(solution)/shard_map/all_to_all | solution.py:201
  242.4 9.3 %fusion.1 = f32[2,32,1024]{2,0,1:T(2,128)S(1)} fusion(f32[32,2,32,1024]{3,1,2,0:T(2,128)} %mul.137, bf16[2,32,32,1024]{3,0,2,1:T(2,128)(2,1)} %bitcast.9), kind=kLoop, calls=%fused_computation.2 | loop fusion | flops 6225920 | bytes 12845056 | tf_op jit(solution)/shard_map/reduce_sum | solution.py:209
  251.7 0.1 divide_convert_fusion
  251.9 0.7 copy.21
  (32 shorter events, 1.0 us)
Async XLA Ops:
  7.2 34.1 %copy-start.4 = (s32[2]{0:T(128)S(1)}, s32[2]{0:T(128)}, u32[]{:S(2)}) copy-start(s32[2]{0:T(128)} %param.15) | copy-start | bytes 28
  7.2 88.3 %all-gather.3.cloned.1.call-start = ((), (), s32[]{:S(2)}) async-start(), calls=%async_computation.2 | async-start | bytes 8650752 | tf_op jit(solution)/shard_map/all_gather | solution.py:164
  37.7 114.8 %all-gather.5.cloned.1.call-start = ((), (), s32[]{:S(2)}) async-start(), calls=%async_computation.3 | async-start | bytes 4325376 | tf_op jit(solution)/shard_map/all_gather | solution.py:188
  95.5 7.2 %copy-start = (bf16[2,256,512]{2,1,0:T(8,128)(2,1)S(1)}, bf16[2,256,512]{2,1,0:T(8,128)(2,1)}, u32[]{:S(2)}) copy-start(bf16[2,256,512]{2,1,0:T(8,128)(2,1)} %param.14) | copy-start | bytes 1572868
  95.5 7.2 %copy-start.1 = (bf16[2,256,512]{2,1,0:T(8,128)(2,1)S(1)}, bf16[2,256,512]{2,1,0:T(8,128)(2,1)}, u32[]{:S(2)}) copy-start(bf16[2,256,512]{2,1,0:T(8,128)(2,1)} %param.13) | copy-start | bytes 1572868
  102.3 60.6 %copy-start.2 = (bf16[64,512]{1,0:T(8,128)(2,1)}, bf16[64,512]{1,0:T(8,128)(2,1)S(1)}, u32[]{:S(2)}) copy-start(bf16[64,512]{1,0:T(8,128)(2,1)S(1)} %slice.64) | copy-start | bytes 196612
  102.7 60.3 %copy-start.3 = (bf16[2,32,512]{2,1,0:T(8,128)(2,1)}, bf16[2,32,512]{2,1,0:T(8,128)(2,1)S(1)}, u32[]{:S(2)}) copy-start(bf16[2,32,512]{2,1,0:T(8,128)(2,1)S(1)} %convert_element_type.42) | copy-start | bytes 196612
  167.2 13.9 %all-to-all-start.1 = ((f32[32,1,512]{2,1,0:T(1,128)}), f32[32,1,512]{2,1,0:T(1,128)S(1)}, u32[]{:S(2)}, u32[]{:S(2)}) async-start(f32[32,1,512]{2,1,0:T(1,128)} %reshape.81), calls=%async_computation.1 | async-start | bytes 131072 | tf_op jit(solution)/shard_map/all_to_all | solution.py:200
  181.1 61.3 %all-to-all-start = ((bf16[2,1024,1024]{2,0,1:T(2,128)(2,1)}), bf16[2,1024,1024]{2,0,1:T(2,128)(2,1)}, u32[]{:S(2)}, u32[]{:S(2)}) async-start(bf16[2,1024,1024]{2,0,1:T(2,128)(2,1)} %copy.19), calls=%async_computation | async-start | bytes 8388608 | tf_op jit(solution)/shard_map/all_to_all | solution.py:201
Sparse Core Ops, SparseCore 0:
  37.8 57.6 all-gather.2
  101.7 50.6 all-gather.4

commit v3 on v2

--- a/solution.py
+++ b/solution.py
@@ -37,55 +37,13 @@
     )
 
 
-def attend(query_rows, key_rows, value_rows, live):
-    span_len = query_rows.shape[0]
-    group_size = HEADS // KV_HEADS
-    query_view = query_rows.reshape(span_len, KV_HEADS, group_size, HEAD)
-    key_view = key_rows.reshape(key_rows.shape[0], KV_HEADS, HEAD)
-    value_view = value_rows.reshape(value_rows.shape[0], KV_HEADS, HEAD)
-    scores = jnp.einsum(
-        "cgeh,kgh->cgek", query_view, key_view, preferred_element_type=jnp.float32
-    ) * HEAD ** (-0.5)
-    mask_view = live[:, None, None, :]
-    scores = jnp.where(mask_view, scores, MASKED)
-    block_max = jnp.max(scores, axis=-1)
-    weights = jnp.where(mask_view, jnp.exp(scores - block_max[..., None]), 0.0)
-    block_sum = jnp.sum(weights, axis=-1)
-    block_out = jnp.einsum(
-        "cgek,kgh->cgeh",
-        weights.astype(jnp.bfloat16),
-        value_view,
-        preferred_element_type=jnp.float32,
-    )
-    return (
-        block_max.reshape(span_len, HEADS),
-        block_sum.reshape(span_len, HEADS),
-        block_out.reshape(span_len, HEADS * HEAD).astype(jnp.bfloat16),
-    )
-
-
-def attend_rows(query_rows, key_rows, value_rows, live):
-    total_rows = query_rows.shape[0]
-    row_block = min(512, total_rows)
-    pieces = []
-    for begin in range(0, total_rows, row_block):
-        pieces.append(
-            attend(
-                query_rows[begin : begin + row_block],
-                key_rows,
-                value_rows,
-                live[begin : begin + row_block],
-            )
-        )
-    return tuple((jnp.concatenate([piece[slot] for piece in pieces], axis=0) for slot in range(3)))
-
-
 def attention_kernel(scalar_ref, query_ref, key_ref, value_ref, stats_ref, out_ref, *, cache_len_dev, slice_len):
     request = pl.program_id(0)
     length = scalar_ref[request]
     seat = scalar_ref[scalar_ref.shape[0] - 1]
     span_len = query_ref.shape[1]
     key_rows = key_ref.shape[1]
+    blocks = out_ref.shape[0]
     key_index = lax.broadcasted_iota(jnp.int32, (span_len, key_rows), 1)
     query_index = lax.broadcasted_iota(jnp.int32, (span_len, key_rows), 0)
     cache_live = seat * cache_len_dev + key_index < length
@@ -111,16 +69,19 @@
         block_out = jnp.dot(
             weights.astype(jnp.bfloat16), value_rows_h, preferred_element_type=jnp.float32
         )
-        out_ref[0, :, head * HEAD : (head + 1) * HEAD] = block_out.astype(jnp.bfloat16)
+        out_ref[:, 0, :, head * HEAD : (head + 1) * HEAD] = block_out.astype(jnp.bfloat16).reshape(
+            blocks, span_len // blocks, HEAD
+        )
         stats = jnp.where(lane == head, block_max, stats)
         stats = jnp.where(lane == HEADS + head, block_sum, stats)
-    stats_ref[0] = stats
-
-
-def block_attention(all_queries, key_block, value_block, scalars, cache_len_dev, slice_len):
+    stats_ref[:, 0] = stats[:, : stats_ref.shape[3]].reshape(blocks, span_len // blocks, stats_ref.shape[3])
+
+
+def block_attention(all_queries, key_block, value_block, scalars, cache_len_dev, slice_len, blocks):
     req_local, span_len, query_width = all_queries.shape
     key_rows = key_block.shape[1]
     kv_width = key_block.shape[2]
+    chunk = span_len // blocks
     grid_spec = pltpu.PrefetchScalarGridSpec(
         num_scalar_prefetch=1,
         grid=(req_local,),
@@ -130,18 +91,66 @@
             pl.BlockSpec((1, key_rows, kv_width), lambda r, s: (r, 0, 0)),
         ],
         out_specs=[
-            pl.BlockSpec((1, span_len, 128), lambda r, s: (r, 0, 0)),
-            pl.BlockSpec((1, span_len, query_width), lambda r, s: (r, 0, 0)),
+            pl.BlockSpec((blocks, 1, chunk, 2 * HEADS), lambda r, s: (0, r, 0, 0)),
+            pl.BlockSpec((blocks, 1, chunk, query_width), lambda r, s: (0, r, 0, 0)),
         ],
     )
     return pl.pallas_call(
         functools.partial(attention_kernel, cache_len_dev=cache_len_dev, slice_len=slice_len),
         grid_spec=grid_spec,
         out_shape=[
-            jax.ShapeDtypeStruct((req_local, span_len, 128), jnp.float32),
-            jax.ShapeDtypeStruct((req_local, span_len, query_width), jnp.bfloat16),
+            jax.ShapeDtypeStruct((blocks, req_local, chunk, 2 * HEADS), jnp.float32),
+            jax.ShapeDtypeStruct((blocks, req_local, chunk, query_width), jnp.bfloat16),
         ],
     )(scalars, all_queries, key_block, value_block)
+
+
+def combine_kernel(stats_ref, out_ref, result_ref):
+    blocks, _, chunk, stat_width = stats_ref.shape
+    width = out_ref.shape[3]
+    top = stats_ref[0, 0]
+    for block in range(1, blocks):
+        top = jnp.maximum(top, stats_ref[block, 0])
+    lane = lax.broadcasted_iota(jnp.int32, (chunk, stat_width), 1)
+
+    def step(block, carry):
+        summed, total = carry
+        row_stats = stats_ref[block, 0]
+        factor = jnp.exp(row_stats - top)
+        rows = out_ref[block, 0].astype(jnp.float32)
+        pieces = []
+        new_total = []
+        for head in range(HEADS):
+            head_factor = jnp.sum(jnp.where(lane == head, factor, 0.0), axis=1, keepdims=True)
+            head_sum = jnp.sum(jnp.where(lane == HEADS + head, row_stats, 0.0), axis=1, keepdims=True)
+            pieces.append(summed[head] + rows[:, head * HEAD : (head + 1) * HEAD] * head_factor)
+            new_total.append(total[head] + head_factor * head_sum)
+        return (tuple(pieces), tuple(new_total))
+
+    start = (
+        tuple(jnp.zeros((chunk, HEAD), jnp.float32) for _ in range(HEADS)),
+        tuple(jnp.zeros((chunk, 1), jnp.float32) for _ in range(HEADS)),
+    )
+    summed, total = lax.fori_loop(0, blocks, step, start)
+    for head in range(HEADS):
+        result_ref[0, :, head * HEAD : (head + 1) * HEAD] = (summed[head] / total[head]).astype(
+            result_ref.dtype
+        )
+
+
+def combine(got_stats, got_out):
+    blocks, req_local, chunk, stat_width = got_stats.shape
+    width = got_out.shape[3]
+    return pl.pallas_call(
+        combine_kernel,
+        grid=(req_local,),
+        in_specs=[
+            pl.BlockSpec((blocks, 1, chunk, stat_width), lambda r: (0, r, 0, 0)),
+            pl.BlockSpec((blocks, 1, chunk, width), lambda r: (0, r, 0, 0)),
+        ],
+        out_specs=pl.BlockSpec((1, chunk, width), lambda r: (r, 0, 0)),
+        out_shape=jax.ShapeDtypeStruct((req_local, chunk, width), jnp.bfloat16),
+    )(got_stats, got_out)
 
 
 def body(hidden_in, norm_gain, w_query, w_key, w_value, cache_keys, cache_values, cache_lengths):
@@ -195,23 +204,12 @@
         axis=1,
     )
     scalars = jnp.concatenate([cache_lengths.astype(jnp.int32), seq_seat.astype(jnp.int32)[None]])
-    stats, out_all = block_attention(all_queries, key_block, value_block, scalars, cache_len_dev, slice_len)
-    stats = stats[:, :, : 2 * HEADS]
-    got_stats = lax.all_to_all(stats, "seq", split_axis=1, concat_axis=0, tiled=True)
-    got_out = lax.all_to_all(out_all, "seq", split_axis=1, concat_axis=0, tiled=True)
-    got_stats = got_stats.reshape(seq_count, req_local, slice_len, 2 * HEADS)
-    got_max = got_stats[..., :HEADS]
-    got_sum = got_stats[..., HEADS:]
-    got_out = got_out.reshape(seq_count, req_local, slice_len, HEADS, HEAD)
-    best_max = jnp.max(got_max, axis=0)
-    factor = jnp.exp(got_max - best_max)
-    total_sum = jnp.sum(got_sum * factor, axis=0)
-    total_out = jnp.sum(got_out.astype(jnp.float32) * factor[..., None], axis=0)
-    attended = (
-        (total_out / total_sum[..., None])
-        .reshape(req_local, slice_len, HEADS * HEAD)
-        .astype(jnp.bfloat16)
-    )
+    stats, out_all = block_attention(
+        all_queries, key_block, value_block, scalars, cache_len_dev, slice_len, seq_count
+    )
+    got_stats = lax.all_to_all(stats, "seq", split_axis=0, concat_axis=0, tiled=True)
+    got_out = lax.all_to_all(out_all, "seq", split_axis=0, concat_axis=0, tiled=True)
+    attended = combine(got_stats, got_out)
     return (attended, new_keys, new_values)
 
 

time: 260 us -> 254 us (0.977)
  local copies, waits for them, and re-layouts: 34.7 us -> 6.26 us
  waiting for transfers between devices: 135 us -> 153 us
  blocking collectives: 29.7 us -> 42.2 us
  other arithmetic: 17.6 us -> 6.34 us
  Pallas kernels: 10.5 us -> 20.8 us
  starting transfers between devices: 12.8 us -> 4.94 us
    all_to_all x2 -> x1, waiting for transfers between devices: 32.5 us -> 51.1 us  [body(): lax.all_to_all(out_all, 'seq', split_axis=0, concat_axis=0, tiled=True)]
    mul x2 -> x0, local copies, waits for them, and re-layouts: 16.3 us -> none  [body(): total_out = jnp.sum(got_out.astype(jnp.float32) * factor[..., None], axis=0)]
    all_to_all x0 -> x1, blocking collectives: none -> 12.5 us  [body(): lax.all_to_all(stats, 'seq', split_axis=0, concat_axis=0, tiled=True)]
    reduce_sum x2 -> x0, other arithmetic: 10.7 us -> none  [the longest x1 9.3 us: body(): total_out = jnp.sum(got_out.astype(jnp.float32) * factor[..., None], axis=0)]
    pallas_call x0 -> x1, Pallas kernels: none -> 10.4 us  [combine(): pl.pallas_call(combine_kernel, grid=(req_local,), in_specs=[pl.BlockSpec(...]
    all_to_all x2 -> x1, starting transfers between devices: 12.8 us -> 4.86 us  [body(): lax.all_to_all(out_all, 'seq', split_axis=0, concat_axis=0, tiled=True)]
    pallas_call x1, local copies, waits for them, and re-layouts: 8.44 us -> 1.54 us  [block_attention(): pl.pallas_call(functools.partial(attention_kernel, cache_len_dev=cache_le...]
    unnamed x13 -> x12, local copies, waits for them, and re-layouts: 4.52 us -> 0.32 us
  transfers between devices with their start and end apart: 4 -> 3, of which waited for: 3 -> 3; matrix products, arithmetic and copies ran while one was open for 14% -> 4% of each run, Pallas kernels for 0% -> 0%
where the time goes in v3:
time: 254 us; the launch traced here: 253 us
  waiting for transfers between devices  153 us (60%)
  blocking collectives  42.2 us (17%)
  Pallas kernels  20.8 us (8%)
  between operations  14.3 us (6%)
  other arithmetic  6.34 us (2%)
  local copies, waits for them, and re-layouts  6.26 us (2%)
  matrix products  4.98 us (2%)
  starting transfers between devices  4.94 us (2%)
    all_gather x1, waiting for transfers between devices, body(): joined = lax.all_gather(joined, 'seq', axis=0, tiled=True)  53.9 us
    all_to_all x1, waiting for transfers between devices, body(): lax.all_to_all(out_all, 'seq', split_axis=0, concat_axis=0, tiled=True)  51.1 us
    all_gather x1, waiting for transfers between devices, body(): all_queries = lax.all_gather(queries, 'seq', axis=1, tiled=True)  48.4 us
    all_gather x1, blocking collectives, body(): joined = lax.all_gather(joined, 'req', axis=0, tiled=True)  29.7 us
    all_to_all x1, blocking collectives, body(): lax.all_to_all(stats, 'seq', split_axis=0, concat_axis=0, tiled=True)  12.5 us
    pallas_call x1, Pallas kernels, block_attention(): pl.pallas_call(functools.partial(attention_kernel, cache_len_dev=cache_le...  10.4 us
    pallas_call x1, Pallas kernels, combine(): pl.pallas_call(combine_kernel, grid=(req_local,), in_specs=[pl.BlockSpec(...  10.4 us
  transfers between devices with their start and end apart: 3, of which 3 were waited for; matrix products, arithmetic and copies ran while one was open for 4% of the time, Pallas kernels for 0%

profile of v3, /device:TPU:32, one launch (start us, length us, event | category | flops | bytes accessed | tf_op | source)
XLA Modules:
  0.0 253.1 jit_solution(10785668200136499949)
XLA Ops:
  7.2 0.8 pad_maximum_fusion.2
  8.0 29.7 %all_gather.9 = bf16[64,2048]{1,0:T(8,128)(2,1)} all-gather(bf16[8,2048]{1,0:T(8,128)(2,1)S(1)} %pad_maximum_fusion.2), channel_id=1, replica_groups=mesh['req'=8,'seq'=32] {'req'}, dimensions={0}, use_global_device_ids=true | all-gather | bytes 294912 | tf_op jit(solution)/shard_map/all_gather | solution.py:172
  37.7 1.1 fusion
  38.8 1.1 fusion.2
  39.9 0.7 copy.13
  40.7 0.5 reshape_reshape.3
  41.1 0.1 copy.14
  41.3 0.1 add_convert_fusion.2
  41.4 0.2 multiply_cosine_fusion
  41.6 53.9 %all-gather.3.cloned.1.call-done = bf16[2048,2048]{1,0:T(8,128)(2,1)} async-done(((bf16[64,2048]{1,0:T(8,128)(2,1)}), bf16[2048,2048]{1,0:T(8,128)(2,1)}) %all-gather.3.cloned.1.call-update) | async-done | bytes 8388624 | tf_op jit(solution)/shard_map/all_gather | solution.py:173
  95.5 5.0 %fusion.3 = f32[64,2048]{1,0:T(8,128)S(1)} fusion(bf16[64,2048]{0,1:T(8,128)(2,1)S(1)} %bitcast.10, bf16[2048,2048]{1,0:T(8,128)(2,1)} %all-gather.3.cloned.1.call-done), kind=kOutput, calls=%fused_computation.22 | convolution fusion | flops 536870912 | bytes 9175040 | tf_op jit(solution)/shard_map/dot_general | solution.py:179
  100.5 0.1 reshape.63
  100.6 0.1 subtract_convert_fusion
  100.7 0.1 pad_maximum_fusion
  100.8 0.7 convert_element_type.28
  101.5 0.1 pad.5.clone
  101.6 0.6 pad_add_fusion.scalar_ref
  102.3 0.1 reshape.64
  102.4 0.1 subtract_convert_fusion.1
  102.6 1.4 maximum_maximum_fusion.1
  104.0 48.4 %all-gather.5.cloned.1.call-done.query_ref = bf16[2,1024,1024]{2,1,0:T(8,128)(2,1)} async-done(((bf16[2,32,1024]{2,1,0:T(8,128)(2,1)}), bf16[2,1024,1024]{2,1,0:T(8,128)(2,1)}) %all-gather.5.cloned.1.call-update) | async-done | bytes 4194320 | tf_op jit(solution)/shard_map/all_gather | solution.py:197
  152.4 10.4 %shard_map.103 = (f32[32,2,32,8]{3,2,1,0:T(8,128)}, bf16[32,2,32,1024]{3,2,1,0:T(8,128)(2,1)}) custom-call(s32[3]{0:T(128)} %pad_add_fusion.scalar_ref, bf16[2,1024,1024]{2,1,0:T(8,128)(2,1)} %all-gather.5.cloned.1.call-done.query_ref, bf16[2,384,512]{2,1,0:T(8,128)(2,1)} %get-tuple-element.14.key_ref, bf16[2,384,512]{2,1,0:T(8,128)(2,1)} %get-tuple-element.13.value_ref), custom_call_target="tpu_custom_call" | custom-call | tf_op jit(solution)/shard_map/pallas_call | solution.py:98
  162.8 1.5 copy.15
  164.4 0.2 reshape.65
  164.6 12.5 %all_to_all.10 = f32[32,1,512]{2,1,0:T(1,128)S(1)} all-to-all(f32[32,1,512]{2,1,0:T(1,128)S(1)} %reshape.65), channel_id=1, replica_groups=mesh['req'=8,'seq'=32] {'seq'}, dimensions={0} | all-to-all | bytes 131072 | tf_op jit(solution)/shard_map/all_to_all | solution.py:210
  177.1 4.9 %all-to-all-start.1 = ((bf16[32,2,32,1024]{3,2,1,0:T(8,128)(2,1)}), bf16[32,2,32,1024]{3,2,1,0:T(8,128)(2,1)}, u32[]{:S(2)}, u32[]{:S(2)}) async-start(bf16[32,2,32,1024]{3,2,1,0:T(8,128)(2,1)} %get-tuple-element.6), calls=%async_computation.1 | async-start | bytes 8388608 | tf_op jit(solution)/shard_map/all_to_all | solution.py:211
  182.0 0.5 broadcast.59
  182.5 0.8 reduce
  183.3 0.1 reshape.66
  183.4 1.4 copy.16.stats_ref
  184.8 51.1 %all-to-all-done.1.out_ref = bf16[32,2,32,1024]{3,2,1,0:T(8,128)(2,1)} async-done(((bf16[32,2,32,1024]{3,2,1,0:T(8,128)(2,1)}), bf16[32,2,32,1024]{3,2,1,0:T(8,128)(2,1)}, u32[]{:S(2)}, u32[]{:S(2)}) %all-to-all-start.1) | async-done | bytes 4194336 | tf_op jit(solution)/shard_map/all_to_all | solution.py:211
  235.9 10.4 %shard_map.104 = bf16[2,32,1024]{2,1,0:T(8,128)(2,1)} custom-call(f32[32,2,32,8]{3,2,1,0:T(8,128)} %copy.16.stats_ref, bf16[32,2,32,1024]{3,2,1,0:T(8,128)(2,1)} %all-to-all-done.1.out_ref), custom_call_target="tpu_custom_call" | custom-call | tf_op jit(solution)/shard_map/pallas_call | solution.py:144
  (23 shorter events, 0.3 us)
Async XLA Ops:
  7.2 88.3 %all-gather.3.cloned.1.call-start = ((), (), s32[]{:S(2)}) async-start(), calls=%async_computation.2 | async-start | bytes 8650752 | tf_op jit(solution)/shard_map/all_gather | solution.py:173
  37.6 114.7 %all-gather.5.cloned.1.call-start = ((), (), s32[]{:S(2)}) async-start(), calls=%async_computation.3 | async-start | bytes 4325376 | tf_op jit(solution)/shard_map/all_gather | solution.py:197
  40.6 0.7 copy-start.4
  100.4 2.1 copy-start
  100.5 2.1 copy-start.1
  102.2 1.8 copy-start.2
  102.6 60.3 %copy-start.3 = (bf16[2,32,512]{2,1,0:T(8,128)(2,1)}, bf16[2,32,512]{2,1,0:T(8,128)(2,1)S(1)}, u32[]{:S(2)}) copy-start(bf16[2,32,512]{2,1,0:T(8,128)(2,1)S(1)} %convert_element_type.29) | copy-start | bytes 196612
  177.1 58.8 %all-to-all-start.1 = ((bf16[32,2,32,1024]{3,2,1,0:T(8,128)(2,1)}), bf16[32,2,32,1024]{3,2,1,0:T(8,128)(2,1)}, u32[]{:S(2)}, u32[]{:S(2)}) async-start(bf16[32,2,32,1024]{3,2,1,0:T(8,128)(2,1)} %get-tuple-element.6), calls=%async_computation.1 | async-start | bytes 8388608 | tf_op jit(solution)/shard_map/all_to_all | solution.py:211
Sparse Core Ops, SparseCore 0:
  37.8 57.6 all-gather.2
  101.6 50.6 all-gather.4

commit v4 on v3

--- a/solution.py
+++ b/solution.py
@@ -153,6 +153,19 @@
     )(got_stats, got_out)
 
 
+def gather_by_doubling(rows, axis_name, count):
+    seat = lax.axis_index(axis_name)
+    distance = 1
+    while distance < count:
+        pairs = [(source, source ^ distance) for source in range(count)]
+        other = lax.ppermute(rows, axis_name, pairs)
+        low_first = jnp.concatenate([rows, other], axis=0)
+        high_first = jnp.concatenate([other, rows], axis=0)
+        rows = jnp.where((seat & distance) == 0, low_first, high_first)
+        distance *= 2
+    return rows
+
+
 def body(hidden_in, norm_gain, w_query, w_key, w_value, cache_keys, cache_values, cache_lengths):
     seq_count = lax.axis_size("seq")
     seq_seat = lax.axis_index("seq")
@@ -169,7 +182,7 @@
     query_cols = w_query.shape[1]
     key_cols = w_key.shape[1]
     joined = jnp.concatenate([w_query, w_key, w_value], axis=1)
-    joined = lax.all_gather(joined, "req", axis=0, tiled=True)
+    joined = gather_by_doubling(joined, "req", req_count)
     joined = lax.all_gather(joined, "seq", axis=0, tiled=True)
     permuted_rows = (
         flat_rows.reshape(-1, req_count, seq_count, row_local)

time: 254 us -> 248 us (0.976)
  blocking collectives: 42.2 us -> 12.5 us
  starting transfers between devices: 4.94 us -> 16.2 us
  waiting for transfers between devices: 153 us -> 164 us
    all_gather x1 -> x0, blocking collectives: 29.7 us -> none  [body(): joined = lax.all_gather(joined, 'req', axis=0, tiled=True)]
    ppermute x0 -> x3, starting transfers between devices: none -> 11.2 us  [gather_by_doubling(): other = lax.ppermute(rows, axis_name, pairs)]
    ppermute x0 -> x3, waiting for transfers between devices: none -> 8 us  [gather_by_doubling(): other = lax.ppermute(rows, axis_name, pairs)]
    all_gather x1, waiting for transfers between devices: 53.9 us -> 56.7 us  [body(): joined = lax.all_gather(joined, 'seq', axis=0, tiled=True)]
  transfers between devices with their start and end apart: 3 -> 6, of which waited for: 3 -> 6; matrix products, arithmetic and copies ran while one was open for 4% -> 4% of each run, Pallas kernels for 0% -> 0%
where the time goes in v4:
time: 248 us
  waiting for transfers between devices  164 us (66%)
  Pallas kernels  20.8 us (8%)
  starting transfers between devices  16.2 us (7%)
  between operations  14.3 us (6%)
  blocking collectives  12.5 us (5%)
  local copies, waits for them, and re-layouts  8.41 us (3%)
  other arithmetic  6.17 us (2%)
  matrix products  4.98 us (2%)
    all_gather x1, waiting for transfers between devices, body(): joined = lax.all_gather(joined, 'seq', axis=0, tiled=True)  56.7 us
    all_to_all x1, waiting for transfers between devices, body(): lax.all_to_all(out_all, 'seq', split_axis=0, concat_axis=0, tiled=True)  51.1 us
    all_gather x1, waiting for transfers between devices, body(): all_queries = lax.all_gather(queries, 'seq', axis=1, tiled=True)  48.3 us
    all_to_all x1, blocking collectives, body(): lax.all_to_all(stats, 'seq', split_axis=0, concat_axis=0, tiled=True)  12.5 us
    ppermute x3, starting transfers between devices, gather_by_doubling(): other = lax.ppermute(rows, axis_name, pairs)  11.2 us
    pallas_call x1, Pallas kernels, block_attention(): pl.pallas_call(functools.partial(attention_kernel, cache_len_dev=cache_le...  10.4 us
    pallas_call x1, Pallas kernels, combine(): pl.pallas_call(combine_kernel, grid=(req_local,), in_specs=[pl.BlockSpec(...  10.4 us
    ppermute x3, waiting for transfers between devices, gather_by_doubling(): other = lax.ppermute(rows, axis_name, pairs)  8 us
  transfers between devices with their start and end apart: 6, of which 6 were waited for; matrix products, arithmetic and copies ran while one was open for 4% of the time, Pallas kernels for 0%

profile of v4, /device:TPU:32, one launch (start us, length us, event | category | flops | bytes accessed | tf_op | source)
XLA Modules:
  0.0 247.5 jit_solution(2276295158848887640)
XLA Ops:
  7.2 0.8 constant_dynamic-update-slice_fusion.2
  8.0 0.7 constant_dynamic-update-slice_fusion.1
  8.7 0.7 constant_dynamic-update-slice_fusion
  9.4 1.8 collective-permute-start
  11.2 2.1 collective-permute-done
  13.3 3.4 %collective-permute-start.1 = (bf16[16,2048]{1,0:T(8,128)(2,1)S(1)}, bf16[16,2048]{1,0:T(8,128)(2,1)S(1)}, u32[]{:S(2)}, u32[]{:S(2)}) collective-permute-start(bf16[16,2048]{1,0:T(8,128)(2,1)S(1)} %maximum_select_fusion.2), channel_id=1, source_target_pairs={{0,64},{32,96},{64,0},{96,32},{128,192},{160,224},{192,128},{224,1... | collective-permute-start | bytes 196616 | tf_op jit(solution)/shard_map/ppermute | solution.py:161
  16.7 2.3 collective-permute-done.1
  19.0 6.1 %collective-permute-start.2 = (bf16[32,2048]{1,0:T(8,128)(2,1)S(1)}, bf16[32,2048]{1,0:T(8,128)(2,1)S(1)}, u32[]{:S(2)}, u32[]{:S(2)}) collective-permute-start(bf16[32,2048]{1,0:T(8,128)(2,1)S(1)} %maximum_select_fusion.1), channel_id=1, source_target_pairs={{0,128},{32,160},{64,192},{96,224},{128,0},{160,32},{192,64},{224,... | collective-permute-start | bytes 393224 | tf_op jit(solution)/shard_map/ppermute | solution.py:161
  25.1 3.6 %collective-permute-done.2 = bf16[32,2048]{1,0:T(8,128)(2,1)S(1)} collective-permute-done((bf16[32,2048]{1,0:T(8,128)(2,1)S(1)}, bf16[32,2048]{1,0:T(8,128)(2,1)S(1)}, u32[]{:S(2)}, u32[]{:S(2)}) %collective-permute-start.2) | collective-permute-done | bytes 131104 | tf_op jit(solution)/shard_map/ppermute | solution.py:161
  28.6 0.8 maximum_select_fusion
  29.5 1.1 fusion
  30.6 0.8 fusion.2
  31.4 0.7 copy.13
  32.2 0.5 reshape_reshape.3
  32.7 0.1 copy.14
  32.9 0.2 multiply_cosine_fusion
  33.1 56.7 %all-gather.3.cloned.1.call-done = bf16[2048,2048]{1,0:T(8,128)(2,1)} async-done(((bf16[64,2048]{1,0:T(8,128)(2,1)}), bf16[2048,2048]{1,0:T(8,128)(2,1)}) %all-gather.3.cloned.1.call-update) | async-done | bytes 8388624 | tf_op jit(solution)/shard_map/all_gather | solution.py:186
  89.8 5.0 %fusion.3 = f32[64,2048]{1,0:T(8,128)S(1)} fusion(bf16[64,2048]{0,1:T(8,128)(2,1)S(1)} %bitcast.10, bf16[2048,2048]{1,0:T(8,128)(2,1)} %all-gather.3.cloned.1.call-done), kind=kOutput, calls=%fused_computation.27 | convolution fusion | flops 536870912 | bytes 9175040 | tf_op jit(solution)/shard_map/dot_general | solution.py:192
  95.2 0.7 convert_element_type.28
  96.0 0.7 pad_add_fusion.scalar_ref
  97.0 1.4 maximum_maximum_fusion.1
  98.5 48.3 %all-gather.5.cloned.1.call-done.query_ref = bf16[2,1024,1024]{2,1,0:T(8,128)(2,1)} async-done(((bf16[2,32,1024]{2,1,0:T(8,128)(2,1)}), bf16[2,1024,1024]{2,1,0:T(8,128)(2,1)}) %all-gather.5.cloned.1.call-update) | async-done | bytes 4194320 | tf_op jit(solution)/shard_map/all_gather | solution.py:210
  146.8 10.4 %shard_map.103 = (f32[32,2,32,8]{3,2,1,0:T(8,128)}, bf16[32,2,32,1024]{3,2,1,0:T(8,128)(2,1)}) custom-call(s32[3]{0:T(128)} %pad_add_fusion.scalar_ref, bf16[2,1024,1024]{2,1,0:T(8,128)(2,1)} %all-gather.5.cloned.1.call-done.query_ref, bf16[2,384,512]{2,1,0:T(8,128)(2,1)} %get-tuple-element.14.key_ref, bf16[2,384,512]{2,1,0:T(8,128)(2,1)} %get-tuple-element.13.value_ref), custom_call_target="tpu_custom_call" | custom-call | tf_op jit(solution)/shard_map/pallas_call | solution.py:98
  157.2 1.5 copy.15
  158.8 0.2 reshape.65
  158.9 12.5 %all_to_all.10 = f32[32,1,512]{2,1,0:T(1,128)S(1)} all-to-all(f32[32,1,512]{2,1,0:T(1,128)S(1)} %reshape.65), channel_id=1, replica_groups=mesh['req'=8,'seq'=32] {'seq'}, dimensions={0} | all-to-all | bytes 131072 | tf_op jit(solution)/shard_map/all_to_all | solution.py:223
  171.5 4.9 %all-to-all-start.1 = ((bf16[32,2,32,1024]{3,2,1,0:T(8,128)(2,1)}), bf16[32,2,32,1024]{3,2,1,0:T(8,128)(2,1)}, u32[]{:S(2)}, u32[]{:S(2)}) async-start(bf16[32,2,32,1024]{3,2,1,0:T(8,128)(2,1)} %get-tuple-element.6), calls=%async_computation.1 | async-start | bytes 8388608 | tf_op jit(solution)/shard_map/all_to_all | solution.py:224
  176.3 0.5 broadcast.59
  176.9 0.8 reduce
  177.8 1.4 copy.16.stats_ref
  179.2 51.1 %all-to-all-done.1.out_ref = bf16[32,2,32,1024]{3,2,1,0:T(8,128)(2,1)} async-done(((bf16[32,2,32,1024]{3,2,1,0:T(8,128)(2,1)}), bf16[32,2,32,1024]{3,2,1,0:T(8,128)(2,1)}, u32[]{:S(2)}, u32[]{:S(2)}) %all-to-all-start.1) | async-done | bytes 4194336 | tf_op jit(solution)/shard_map/all_to_all | solution.py:224
  230.3 10.4 %shard_map.104 = bf16[2,32,1024]{2,1,0:T(8,128)(2,1)} custom-call(f32[32,2,32,8]{3,2,1,0:T(8,128)} %copy.16.stats_ref, bf16[32,2,32,1024]{3,2,1,0:T(8,128)(2,1)} %all-to-all-done.1.out_ref), custom_call_target="tpu_custom_call" | custom-call | tf_op jit(solution)/shard_map/pallas_call | solution.py:144
  (35 shorter events, 1.1 us)
Async XLA Ops:
  7.2 23.4 %copy-start = (bf16[2,32,2048]{2,1,0:T(8,128)(2,1)S(1)}, bf16[2,32,2048]{2,1,0:T(8,128)(2,1)}, u32[]{:S(2)}) copy-start(bf16[2,32,2048]{2,1,0:T(8,128)(2,1)} %param.8) | copy-start | bytes 786436
  7.2 82.7 %all-gather.3.cloned.1.call-start = ((), (), s32[]{:S(2)}) async-start(), calls=%async_computation.2 | async-start | bytes 8650752 | tf_op jit(solution)/shard_map/all_gather | solution.py:186
  9.4 3.9 %collective-permute-start = (bf16[8,2048]{1,0:T(8,128)(2,1)S(1)}, bf16[8,2048]{1,0:T(8,128)(2,1)S(1)}, u32[]{:S(2)}, u32[]{:S(2)}) collective-permute-start(bf16[8,2048]{1,0:T(8,128)(2,1)S(1)} %constant_dynamic-update-slice_fusion), channel_id=1, source_target_pairs={{0,32},{32,0},{64,96},{96,64},{128,160},{160,128},{192,224},{224,1... | collective-permute-start | bytes 98312 | tf_op jit(solution)/shard_map/ppermute | solution.py:161
  13.3 5.7 %collective-permute-start.1 = (bf16[16,2048]{1,0:T(8,128)(2,1)S(1)}, bf16[16,2048]{1,0:T(8,128)(2,1)S(1)}, u32[]{:S(2)}, u32[]{:S(2)}) collective-permute-start(bf16[16,2048]{1,0:T(8,128)(2,1)S(1)} %maximum_select_fusion.2), channel_id=1, source_target_pairs={{0,64},{32,96},{64,0},{96,32},{128,192},{160,224},{192,128},{224,1... | collective-permute-start | bytes 196616 | tf_op jit(solution)/shard_map/ppermute | solution.py:161
  19.0 9.6 %collective-permute-start.2 = (bf16[32,2048]{1,0:T(8,128)(2,1)S(1)}, bf16[32,2048]{1,0:T(8,128)(2,1)S(1)}, u32[]{:S(2)}, u32[]{:S(2)}) collective-permute-start(bf16[32,2048]{1,0:T(8,128)(2,1)S(1)} %maximum_select_fusion.1), channel_id=1, source_target_pairs={{0,128},{32,160},{64,192},{96,224},{128,0},{160,32},{192,64},{224,... | collective-permute-start | bytes 393224 | tf_op jit(solution)/shard_map/ppermute | solution.py:161
  29.4 117.3 %all-gather.5.cloned.1.call-start = ((), (), s32[]{:S(2)}) async-start(), calls=%async_computation.3 | async-start | bytes 4325376 | tf_op jit(solution)/shard_map/all_gather | solution.py:210
  32.2 0.7 copy-start.5
  94.8 2.2 copy-start.1
  94.8 2.2 copy-start.2
  96.7 1.8 copy-start.3
  97.0 60.2 %copy-start.4 = (bf16[2,32,512]{2,1,0:T(8,128)(2,1)}, bf16[2,32,512]{2,1,0:T(8,128)(2,1)S(1)}, u32[]{:S(2)}) copy-start(bf16[2,32,512]{2,1,0:T(8,128)(2,1)S(1)} %convert_element_type.29) | copy-start | bytes 196612
  171.5 58.8 %all-to-all-start.1 = ((bf16[32,2,32,1024]{3,2,1,0:T(8,128)(2,1)}), bf16[32,2,32,1024]{3,2,1,0:T(8,128)(2,1)}, u32[]{:S(2)}, u32[]{:S(2)}) async-start(bf16[32,2,32,1024]{3,2,1,0:T(8,128)(2,1)} %get-tuple-element.6), calls=%async_computation.1 | async-start | bytes 8388608 | tf_op jit(solution)/shard_map/all_to_all | solution.py:224
Sparse Core Ops, SparseCore 0:
  29.5 60.2 all-gather.2
  96.0 50.6 all-gather.4

commit v5 on v4

--- a/solution.py
+++ b/solution.py
@@ -37,7 +37,7 @@
     )
 
 
-def attention_kernel(scalar_ref, query_ref, key_ref, value_ref, stats_ref, out_ref, *, cache_len_dev, slice_len):
+def attention_kernel(scalar_ref, query_ref, key_ref, value_ref, out_ref, *, cache_len_dev, slice_len):
     request = pl.program_id(0)
     length = scalar_ref[request]
     seat = scalar_ref[scalar_ref.shape[0] - 1]
@@ -74,7 +74,23 @@
         )
         stats = jnp.where(lane == head, block_max, stats)
         stats = jnp.where(lane == HEADS + head, block_sum, stats)
-    stats_ref[:, 0] = stats[:, : stats_ref.shape[3]].reshape(blocks, span_len // blocks, stats_ref.shape[3])
+    first = stats.astype(jnp.bfloat16).astype(jnp.float32)
+    rest = stats - first
+    second = rest.astype(jnp.bfloat16).astype(jnp.float32)
+    third = (rest - second).astype(jnp.bfloat16).astype(jnp.float32)
+    width = 2 * HEADS
+    packed = jnp.where(
+        lane < width,
+        first,
+        jnp.where(
+            lane < 2 * width,
+            pltpu.roll(second, width, 1),
+            jnp.where(lane < 3 * width, pltpu.roll(third, 2 * width, 1), 0.0),
+        ),
+    )
+    out_ref[:, 0, :, HEADS * HEAD :] = packed.astype(jnp.bfloat16).reshape(
+        blocks, span_len // blocks, 128
+    )
 
 
 def block_attention(all_queries, key_block, value_block, scalars, cache_len_dev, slice_len, blocks):
@@ -90,40 +106,41 @@
             pl.BlockSpec((1, key_rows, kv_width), lambda r, s: (r, 0, 0)),
             pl.BlockSpec((1, key_rows, kv_width), lambda r, s: (r, 0, 0)),
         ],
-        out_specs=[
-            pl.BlockSpec((blocks, 1, chunk, 2 * HEADS), lambda r, s: (0, r, 0, 0)),
-            pl.BlockSpec((blocks, 1, chunk, query_width), lambda r, s: (0, r, 0, 0)),
-        ],
+        out_specs=pl.BlockSpec((blocks, 1, chunk, query_width + 128), lambda r, s: (0, r, 0, 0)),
     )
     return pl.pallas_call(
         functools.partial(attention_kernel, cache_len_dev=cache_len_dev, slice_len=slice_len),
         grid_spec=grid_spec,
-        out_shape=[
-            jax.ShapeDtypeStruct((blocks, req_local, chunk, 2 * HEADS), jnp.float32),
-            jax.ShapeDtypeStruct((blocks, req_local, chunk, query_width), jnp.bfloat16),
-        ],
+        out_shape=jax.ShapeDtypeStruct((blocks, req_local, chunk, query_width + 128), jnp.bfloat16),
     )(scalars, all_queries, key_block, value_block)
 
 
-def combine_kernel(stats_ref, out_ref, result_ref):
-    blocks, _, chunk, stat_width = stats_ref.shape
-    width = out_ref.shape[3]
-    top = stats_ref[0, 0]
+def combine_kernel(out_ref, result_ref):
+    blocks, _, chunk, padded = out_ref.shape
+    width = HEADS * HEAD
+    stat_width = 2 * HEADS
+    lane = lax.broadcasted_iota(jnp.int32, (chunk, 128), 1)
+
+    def block_stats(block):
+        packed = out_ref[block, 0, :, width:].astype(jnp.float32)
+        return (packed + pltpu.roll(packed, 128 - stat_width, 1)) + pltpu.roll(packed, 128 - 2 * stat_width, 1)
+
+    top = block_stats(0)
     for block in range(1, blocks):
-        top = jnp.maximum(top, stats_ref[block, 0])
-    lane = lax.broadcasted_iota(jnp.int32, (chunk, stat_width), 1)
+        top = jnp.maximum(top, block_stats(block))
+    top = jnp.where(lane < HEADS, top, 0.0)
 
     def step(block, carry):
         summed, total = carry
-        row_stats = stats_ref[block, 0]
-        factor = jnp.exp(row_stats - top)
-        rows = out_ref[block, 0].astype(jnp.float32)
+        row_stats = block_stats(block)
+        factor = jnp.exp(jnp.where(lane < HEADS, row_stats, 0.0) - top)
         pieces = []
         new_total = []
         for head in range(HEADS):
             head_factor = jnp.sum(jnp.where(lane == head, factor, 0.0), axis=1, keepdims=True)
             head_sum = jnp.sum(jnp.where(lane == HEADS + head, row_stats, 0.0), axis=1, keepdims=True)
-            pieces.append(summed[head] + rows[:, head * HEAD : (head + 1) * HEAD] * head_factor)
+            rows = out_ref[block, 0, :, head * HEAD : (head + 1) * HEAD].astype(jnp.float32)
+            pieces.append(summed[head] + rows * head_factor)
             new_total.append(total[head] + head_factor * head_sum)
         return (tuple(pieces), tuple(new_total))
 
@@ -138,19 +155,16 @@
         )
 
 
-def combine(got_stats, got_out):
-    blocks, req_local, chunk, stat_width = got_stats.shape
-    width = got_out.shape[3]
+def combine(got_out):
+    blocks, req_local, chunk, padded = got_out.shape
+    width = HEADS * HEAD
     return pl.pallas_call(
         combine_kernel,
         grid=(req_local,),
-        in_specs=[
-            pl.BlockSpec((blocks, 1, chunk, stat_width), lambda r: (0, r, 0, 0)),
-            pl.BlockSpec((blocks, 1, chunk, width), lambda r: (0, r, 0, 0)),
-        ],
+        in_specs=[pl.BlockSpec((blocks, 1, chunk, padded), lambda r: (0, r, 0, 0))],
         out_specs=pl.BlockSpec((1, chunk, width), lambda r: (r, 0, 0)),
         out_shape=jax.ShapeDtypeStruct((req_local, chunk, width), jnp.bfloat16),
-    )(got_stats, got_out)
+    )(got_out)
 
 
 def gather_by_doubling(rows, axis_name, count):
@@ -217,12 +231,11 @@
         axis=1,
     )
     scalars = jnp.concatenate([cache_lengths.astype(jnp.int32), seq_seat.astype(jnp.int32)[None]])
-    stats, out_all = block_attention(
+    out_all = block_attention(
         all_queries, key_block, value_block, scalars, cache_len_dev, slice_len, seq_count
     )
-    got_stats = lax.all_to_all(stats, "seq", split_axis=0, concat_axis=0, tiled=True)
     got_out = lax.all_to_all(out_all, "seq", split_axis=0, concat_axis=0, tiled=True)
-    attended = combine(got_stats, got_out)
+    attended = combine(got_out)
     return (attended, new_keys, new_values)
 
 

time: 248 us -> 245 us (0.988)
  waiting for transfers between devices: 164 us -> 113 us
  blocking collectives: 12.5 us -> 61.9 us
  Pallas kernels: 20.8 us -> 27.2 us
  starting transfers between devices: 16.2 us -> 11.3 us
  local copies, waits for them, and re-layouts: 8.41 us -> 4.65 us
    all_to_all x1 -> x0, waiting for transfers between devices: 51.1 us -> none  [body(): lax.all_to_all(out_all, 'seq', split_axis=0, concat_axis=0, tiled=True)]
    all_to_all x1, blocking collectives: 12.5 us -> 61.9 us  [body(): lax.all_to_all(out_all, 'seq', split_axis=0, concat_axis=0, tiled=True)]
    all_to_all x1 -> x0, starting transfers between devices: 4.87 us -> none  [body(): lax.all_to_all(out_all, 'seq', split_axis=0, concat_axis=0, tiled=True)]
    pallas_call x1, Pallas kernels: 10.4 us -> 15 us  [combine(): pl.pallas_call(combine_kernel, grid=(req_local,), in_specs=[pl.BlockSpec(...]
  transfers between devices with their start and end apart: 6 -> 5, of which waited for: 6 -> 5; matrix products, arithmetic and copies ran while one was open for 4% -> 2% of each run, Pallas kernels for 0% -> 0%
where the time goes in v5:
time: 245 us; the launch traced here: 243 us
  waiting for transfers between devices  113 us (46%)
  blocking collectives  61.9 us (25%)
  Pallas kernels  27.2 us (11%)
  between operations  14.3 us (6%)
  starting transfers between devices  11.3 us (5%)
  other arithmetic  5.38 us (2%)
  matrix products  4.98 us (2%)
  local copies, waits for them, and re-layouts  4.65 us (2%)
    all_to_all x1, blocking collectives, body(): lax.all_to_all(out_all, 'seq', split_axis=0, concat_axis=0, tiled=True)  61.9 us
    all_gather x1, waiting for transfers between devices, body(): joined = lax.all_gather(joined, 'seq', axis=0, tiled=True)  56.7 us
    all_gather x1, waiting for transfers between devices, body(): all_queries = lax.all_gather(queries, 'seq', axis=1, tiled=True)  48.3 us
    pallas_call x1, Pallas kernels, combine(): pl.pallas_call(combine_kernel, grid=(req_local,), in_specs=[pl.BlockSpec(...  15 us
    pallas_call x1, Pallas kernels, block_attention(): pl.pallas_call(functools.partial(attention_kernel, cache_len_dev=cache_le...  12.3 us
    ppermute x3, starting transfers between devices, gather_by_doubling(): other = lax.ppermute(rows, axis_name, pairs)  11.2 us
    ppermute x3, waiting for transfers between devices, gather_by_doubling(): other = lax.ppermute(rows, axis_name, pairs)  8 us
    dot_general x1, matrix products, body(): jnp.dot(permuted_rows, joined, preferred_element_type=jnp.float32)  4.98 us
  transfers between devices with their start and end apart: 5, of which 5 were waited for; matrix products, arithmetic and copies ran while one was open for 2% of the time, Pallas kernels for 0%

profile of v5, /device:TPU:32, one launch (start us, length us, event | category | flops | bytes accessed | tf_op | source)
XLA Modules:
  0.0 242.8 jit_solution(14740973157167229898)
XLA Ops:
  7.2 0.8 constant_dynamic-update-slice_fusion.2
  8.0 0.7 constant_dynamic-update-slice_fusion.1
  8.7 0.7 constant_dynamic-update-slice_fusion
  9.4 1.8 collective-permute-start
  11.2 2.1 collective-permute-done
  13.3 3.4 %collective-permute-start.1 = (bf16[16,2048]{1,0:T(8,128)(2,1)S(1)}, bf16[16,2048]{1,0:T(8,128)(2,1)S(1)}, u32[]{:S(2)}, u32[]{:S(2)}) collective-permute-start(bf16[16,2048]{1,0:T(8,128)(2,1)S(1)} %maximum_select_fusion.2), channel_id=1, source_target_pairs={{0,64},{32,96},{64,0},{96,32},{128,192},{160,224},{192,128},{224,1... | collective-permute-start | bytes 196616 | tf_op jit(solution)/shard_map/ppermute | solution.py:175
  16.7 2.3 collective-permute-done.1
  19.0 6.1 %collective-permute-start.2 = (bf16[32,2048]{1,0:T(8,128)(2,1)S(1)}, bf16[32,2048]{1,0:T(8,128)(2,1)S(1)}, u32[]{:S(2)}, u32[]{:S(2)}) collective-permute-start(bf16[32,2048]{1,0:T(8,128)(2,1)S(1)} %maximum_select_fusion.1), channel_id=1, source_target_pairs={{0,128},{32,160},{64,192},{96,224},{128,0},{160,32},{192,64},{224,... | collective-permute-start | bytes 393224 | tf_op jit(solution)/shard_map/ppermute | solution.py:175
  25.1 3.6 %collective-permute-done.2 = bf16[32,2048]{1,0:T(8,128)(2,1)S(1)} collective-permute-done((bf16[32,2048]{1,0:T(8,128)(2,1)S(1)}, bf16[32,2048]{1,0:T(8,128)(2,1)S(1)}, u32[]{:S(2)}, u32[]{:S(2)}) %collective-permute-start.2) | collective-permute-done | bytes 131104 | tf_op jit(solution)/shard_map/ppermute | solution.py:175
  28.6 0.8 maximum_select_fusion
  29.5 1.1 fusion
  30.6 0.8 fusion.2
  31.4 0.7 copy.11
  32.2 0.5 reshape_reshape.3
  32.7 0.1 copy.12
  32.8 0.1 add_convert_fusion.2
  32.9 0.2 multiply_cosine_fusion
  33.1 56.7 %all-gather.3.cloned.1.call-done = bf16[2048,2048]{1,0:T(8,128)(2,1)} async-done(((bf16[64,2048]{1,0:T(8,128)(2,1)}), bf16[2048,2048]{1,0:T(8,128)(2,1)}) %all-gather.3.cloned.1.call-update) | async-done | bytes 8388624 | tf_op jit(solution)/shard_map/all_gather | solution.py:200
  89.8 5.0 %fusion.3 = f32[64,2048]{1,0:T(8,128)S(1)} fusion(bf16[64,2048]{0,1:T(8,128)(2,1)S(1)} %bitcast.8, bf16[2048,2048]{1,0:T(8,128)(2,1)} %all-gather.3.cloned.1.call-done), kind=kOutput, calls=%fused_computation.27 | convolution fusion | flops 536870912 | bytes 9175040 | tf_op jit(solution)/shard_map/dot_general | solution.py:206
  94.9 0.1 reshape.63
  95.0 0.1 subtract_convert_fusion
  95.1 0.1 pad_maximum_fusion
  95.2 0.7 convert_element_type.28
  95.9 0.1 pad.5.clone
  96.0 0.7 pad_add_fusion.scalar_ref
  96.7 0.1 reshape.64
  96.8 0.1 subtract_convert_fusion.1
  97.0 1.4 maximum_maximum_fusion.1
  98.5 48.3 %all-gather.5.cloned.1.call-done.query_ref = bf16[2,1024,1024]{2,1,0:T(8,128)(2,1)} async-done(((bf16[2,32,1024]{2,1,0:T(8,128)(2,1)}), bf16[2,1024,1024]{2,1,0:T(8,128)(2,1)}) %all-gather.5.cloned.1.call-update) | async-done | bytes 4194320 | tf_op jit(solution)/shard_map/all_gather | solution.py:224
  146.8 12.3 %shard_map.103 = bf16[32,2,32,1152]{3,2,1,0:T(8,128)(2,1)} custom-call(s32[3]{0:T(128)} %pad_add_fusion.scalar_ref, bf16[2,1024,1024]{2,1,0:T(8,128)(2,1)} %all-gather.5.cloned.1.call-done.query_ref, bf16[2,384,512]{2,1,0:T(8,128)(2,1)} %get-tuple-element.10.key_ref, bf16[2,384,512]{2,1,0:T(8,128)(2,1)} %get-tuple-element.9.value_ref), custom_call_target="tpu_custom_call" | custom-call | tf_op jit(solution)/shard_map/pallas_call | solution.py:111
  159.1 61.9 %all_to_all.5.out_ref = bf16[32,2,32,1152]{3,2,1,0:T(8,128)(2,1)} all-to-all(bf16[32,2,32,1152]{3,2,1,0:T(8,128)(2,1)} %shard_map.103), channel_id=1, replica_groups=mesh['req'=8,'seq'=32] {'seq'}, dimensions={0} | all-to-all | bytes 9437184 | tf_op jit(solution)/shard_map/all_to_all | solution.py:237
  221.0 15.0 %shard_map.104 = bf16[2,32,1024]{2,1,0:T(8,128)(2,1)} custom-call(bf16[32,2,32,1152]{3,2,1,0:T(8,128)(2,1)} %all_to_all.5.out_ref), custom_call_target="tpu_custom_call" | custom-call | tf_op jit(solution)/shard_map/pallas_call | solution.py:161
  (27 shorter events, 0.4 us)
Async XLA Ops:
  7.2 23.4 %copy-start = (bf16[2,32,2048]{2,1,0:T(8,128)(2,1)S(1)}, bf16[2,32,2048]{2,1,0:T(8,128)(2,1)}, u32[]{:S(2)}) copy-start(bf16[2,32,2048]{2,1,0:T(8,128)(2,1)} %param.8) | copy-start | bytes 786436
  7.2 82.7 %all-gather.3.cloned.1.call-start = ((), (), s32[]{:S(2)}) async-start(), calls=%async_computation.1 | async-start | bytes 8650752 | tf_op jit(solution)/shard_map/all_gather | solution.py:200
  9.4 3.9 %collective-permute-start = (bf16[8,2048]{1,0:T(8,128)(2,1)S(1)}, bf16[8,2048]{1,0:T(8,128)(2,1)S(1)}, u32[]{:S(2)}, u32[]{:S(2)}) collective-permute-start(bf16[8,2048]{1,0:T(8,128)(2,1)S(1)} %constant_dynamic-update-slice_fusion), channel_id=1, source_target_pairs={{0,32},{32,0},{64,96},{96,64},{128,160},{160,128},{192,224},{224,1... | collective-permute-start | bytes 98312 | tf_op jit(solution)/shard_map/ppermute | solution.py:175
  13.3 5.7 %collective-permute-start.1 = (bf16[16,2048]{1,0:T(8,128)(2,1)S(1)}, bf16[16,2048]{1,0:T(8,128)(2,1)S(1)}, u32[]{:S(2)}, u32[]{:S(2)}) collective-permute-start(bf16[16,2048]{1,0:T(8,128)(2,1)S(1)} %maximum_select_fusion.2), channel_id=1, source_target_pairs={{0,64},{32,96},{64,0},{96,32},{128,192},{160,224},{192,128},{224,1... | collective-permute-start | bytes 196616 | tf_op jit(solution)/shard_map/ppermute | solution.py:175
  19.0 9.6 %collective-permute-start.2 = (bf16[32,2048]{1,0:T(8,128)(2,1)S(1)}, bf16[32,2048]{1,0:T(8,128)(2,1)S(1)}, u32[]{:S(2)}, u32[]{:S(2)}) collective-permute-start(bf16[32,2048]{1,0:T(8,128)(2,1)S(1)} %maximum_select_fusion.1), channel_id=1, source_target_pairs={{0,128},{32,160},{64,192},{96,224},{128,0},{160,32},{192,64},{224,... | collective-permute-start | bytes 393224 | tf_op jit(solution)/shard_map/ppermute | solution.py:175
  29.4 117.3 %all-gather.5.cloned.1.call-start = ((), (), s32[]{:S(2)}) async-start(), calls=%async_computation.2 | async-start | bytes 4325376 | tf_op jit(solution)/shard_map/all_gather | solution.py:224
  32.2 0.7 copy-start.5
  94.8 2.2 copy-start.1
  94.8 2.2 copy-start.2
  96.7 1.8 copy-start.3
  97.0 62.1 %copy-start.4 = (bf16[2,32,512]{2,1,0:T(8,128)(2,1)}, bf16[2,32,512]{2,1,0:T(8,128)(2,1)S(1)}, u32[]{:S(2)}) copy-start(bf16[2,32,512]{2,1,0:T(8,128)(2,1)S(1)} %convert_element_type.29) | copy-start | bytes 196612
Sparse Core Ops, SparseCore 0:
  29.5 60.2 all-gather.2
  96.0 50.6 all-gather.4
